TPU v7x, 128 devices: a whole 4x4x4 slice. The times are simulated.
128 devices in a mesh: row: 8 (over x, core), col: 16 (over y, z).
Axes of the slice: x: 4, y: 4, z: 4, core: 2. Of those that a mesh axis runs over, the one named last changes fastest.
Arguments:
- kernel: float32 [16384, 16384], P('row', 'col'), as said below
Outputs:
- schur: float32 [16384, 16384], P('row', 'col')
- panels: float32 [16384, 768], P('row')
Inputs may be any that keep to these rules, and one draw needn't show every extreme that they name: kernel is symmetric and positive definite with smallest eigenvalue of order one.
All inputs are finite; a program needn't handle non-finite values.
Results may differ from a plain program's by a relative error of at most 0.00027.
Values sent between devices are 32-bit elements; how exact they have to be, the bound alone decides.
No kernel may reach another device: no remote copies, remote signals or barrier semaphores. Data moves between devices by JAX's collectives and lax.ppermute only.
A program may use at most 128 MiB of HBM per device.

v0:
```python
import jax
import jax.numpy as jnp
from jax import lax
from jax.sharding import PartitionSpec as P

BLOCK = 256
STEPS = 3


def pick(received, index, count, want):
    total = None
    for shift, part in enumerate(received):
        term = jnp.where((index - shift) % count == want, part, jnp.float32(0.0))
        total = term if total is None else total + term
    return total


def gather_corner(kernel, row_index, col_index):
    row_count = lax.axis_size("row")
    col_count = lax.axis_size("col")
    ring = 4
    rings = col_count // ring
    piece = kernel[:BLOCK, :BLOCK]
    heard = [piece]
    for shift in range(1, ring):
        pairs = [
            (a * col_count + b, a * col_count + (b + shift) % ring)
            for a in range(STEPS)
            for b in range(a + 1)
        ]
        heard.append(lax.ppermute(piece, ("row", "col"), pairs))
    bands = []
    for a in range(STEPS):
        band = jnp.concatenate([pick(heard, col_index % ring, ring, b) for b in range(a + 1)], axis=1)
        bands.append(jnp.pad(band, ((0, 0), (0, (STEPS - 1 - a) * BLOCK))))
    groups = [[0], list(range(1, STEPS))]
    blocks = [None] * STEPS
    for group in groups:
        width = (max(group) + 1) * BLOCK
        mine = None
        for a in group:
            term = jnp.where(row_index == a, bands[a][:, :width], jnp.float32(0.0))
            mine = term if mine is None else mine + term
        across = [mine]
        for hop in range(1, rings):
            pairs = [(a * col_count + z, a * col_count + hop * ring + z) for a in group for z in range(ring)]
            across.append(lax.ppermute(mine, ("row", "col"), pairs))
        mine = pick(across, col_index // ring, rings, 0)
        odd = row_index % 2 == 1
        held = mine
        for shift in range(1, row_count // 2):
            pairs = [
                (a * col_count + q, ((a + 2 * shift) % row_count) * col_count + q)
                for a in group
                for q in range(col_count)
            ]
            got = lax.ppermute(mine, ("row", "col"), pairs)
            source = 0 if len(group) == 1 else 2 - row_index % 2
            held = held + jnp.where((row_index - 2 * shift) % row_count == source, got, jnp.float32(0.0))
        pairs = [(p * col_count + q, (p ^ 1) * col_count + q) for p in range(row_count) for q in range(col_count)]
        other = lax.ppermute(held, ("row", "col"), pairs)
        for a in group:
            band = jnp.where(odd == (a % 2 == 1), held, other)
            blocks[a] = [band[:, b * BLOCK:(b + 1) * BLOCK] for b in range(a + 1)]
    return blocks


def gather_columns(kernel, col_index):
    rows = kernel.shape[0]
    mine = col_index < STEPS
    piece = jnp.where(mine, kernel[:, :BLOCK], jnp.float32(0.0))
    band = jnp.zeros((rows, STEPS * BLOCK), jnp.float32)
    band = lax.dynamic_update_slice(band, piece, (0, jnp.minimum(col_index, STEPS - 1) * BLOCK))
    return lax.psum(band, "col")


def gather_rows(kernel, row_index):
    cols = kernel.shape[1]
    mine = row_index < STEPS
    piece = jnp.where(mine, kernel[:BLOCK, :], jnp.float32(0.0))
    band = jnp.zeros((STEPS * BLOCK, cols), jnp.float32)
    band = lax.dynamic_update_slice(band, piece, (jnp.minimum(row_index, STEPS - 1) * BLOCK, 0))
    return lax.psum(band, "row")


def mul(a, b, transpose_b=False):
    dims = (((1,), (1 if transpose_b else 0,)), ((), ()))
    return lax.dot_general(a, b, dims, precision=lax.Precision.HIGHEST, preferred_element_type=jnp.float32)


def factor_block(schur):
    half = schur.shape[0] // 2
    eye = jnp.eye(half, dtype=jnp.float32)
    top = jnp.linalg.cholesky(schur[:half, :half])
    top_inv = jax.scipy.linalg.solve_triangular(top, eye, lower=True)
    side = mul(schur[half:, :half], top_inv, True)
    bottom = jnp.linalg.cholesky(schur[half:, half:] - mul(side, side, True))
    bottom_inv = jax.scipy.linalg.solve_triangular(bottom, eye, lower=True)
    corner = -mul(bottom_inv, mul(side, top_inv))
    zero = jnp.zeros((half, half), jnp.float32)
    factor = jnp.concatenate(
        [jnp.concatenate([top, zero], axis=1), jnp.concatenate([side, bottom], axis=1)], axis=0
    )
    inverse = jnp.concatenate(
        [jnp.concatenate([top_inv, zero], axis=1), jnp.concatenate([corner, bottom_inv], axis=1)], axis=0
    )
    return factor, inverse


def factor_corner(blocks):
    zero = jnp.zeros((BLOCK, BLOCK), jnp.float32)
    lower = [[None] * STEPS for _ in range(STEPS)]
    diag_inv = []
    for k in range(STEPS):
        schur = blocks[k][k]
        for j in range(k):
            schur = schur - mul(lower[k][j], lower[k][j], True)
        lower[k][k], inverse = factor_block(schur)
        diag_inv.append(inverse)
        for i in range(k + 1, STEPS):
            below = blocks[i][k]
            for j in range(k):
                below = below - mul(lower[i][j], lower[k][j], True)
            lower[i][k] = mul(below, diag_inv[k], True)
    inv = [[None] * STEPS for _ in range(STEPS)]
    for i in range(STEPS):
        inv[i][i] = diag_inv[i]
        for j in range(i - 1, -1, -1):
            acc = mul(lower[i][j], inv[j][j])
            for m in range(j + 1, i):
                acc = acc + mul(lower[i][m], inv[m][j])
            inv[i][j] = -mul(diag_inv[i], acc)
    factor = jnp.concatenate(
        [jnp.concatenate([lower[i][j] if j <= i else zero for j in range(STEPS)], axis=1) for i in range(STEPS)], axis=0
    )
    inverse = jnp.concatenate(
        [jnp.concatenate([inv[i][j] if j <= i else zero for j in range(STEPS)], axis=1) for i in range(STEPS)], axis=0
    )
    return factor, inverse


def apply_inverse(band, inverse, axis):
    parts = []
    for j in range(STEPS):
        hi = (j + 1) * BLOCK
        piece = lax.slice_in_dim(band, 0, hi, axis=axis)
        parts.append(lax.dot_general(
            piece, inverse[j * BLOCK:hi, :hi], (((axis,), (1,)), ((), ())),
            precision=lax.Precision.HIGHEST, preferred_element_type=jnp.float32,
        ))
    return jnp.concatenate(parts, axis=1)


def shards(kernel):
    row_count = lax.axis_size("row")
    col_count = lax.axis_size("col")
    row_index = lax.axis_index("row")
    col_index = lax.axis_index("col")
    rows_local, cols_local = kernel.shape
    width = STEPS * BLOCK
    row_ids = jnp.arange(rows_local) // BLOCK * row_count + row_index
    col_ids = jnp.arange(cols_local) // BLOCK * col_count + col_index

    blocks = gather_corner(kernel, row_index, col_index)
    band_cols = gather_columns(kernel, col_index)
    band_rows = gather_rows(kernel, row_index)

    factor, inverse = factor_corner(blocks)
    panels = apply_inverse(band_cols, inverse, 1)
    across = apply_inverse(band_rows, inverse, 0)
    own = lax.dynamic_slice_in_dim(factor, jnp.minimum(row_index, STEPS - 1) * BLOCK, BLOCK, 0)
    head = jnp.where(row_index < STEPS, own, panels[:BLOCK])
    panels = lax.dynamic_update_slice(panels, head, (0, 0))
    update = lax.dot_general(
        panels, across, (((1,), (1,)), ((), ())),
        precision=lax.Precision.HIGHEST, preferred_element_type=jnp.float32,
    )
    keep = (row_ids >= STEPS)[:, None] & (col_ids >= STEPS)[None, :]
    schur = jnp.where(keep, kernel - update, jnp.float32(0.0))
    return (schur, panels)


def solution(mesh):
    return jax.shard_map(
        shards,
        mesh=mesh,
        in_specs=(P("row", "col"),),
        out_specs=(P("row", "col"), P("row", None)),
        check_vma=False,
    )
```

profile of v0, /device:TPU:10, one launch (start us, length us, event | category | flops | bytes accessed | tf_op | source)
XLA Modules:
  0.0 294.4 jit_solution(15747331829333423559)
XLA Ops:
  7.6 1.3 select_dynamic-update-slice_fusion.1
  8.9 1.7 copy-done.3
  10.7 1.0 slice.80
  11.6 0.7 collective-permute-start.2
  12.3 0.7 collective-permute-start.1
  13.0 0.7 collective-permute-start
  13.8 1.1 select_add_fusion.2
  15.0 0.7 collective-permute-start.5
  15.7 1.4 collective-permute-start.4
  17.0 1.4 collective-permute-start.3
  18.4 3.1 %broadcast_in_dim.69 = f32[2048,768]{1,0:T(8,128)} broadcast(f32[]{:T(128)} %constant.247.clone.1), dimensions={} | broadcast | bytes 6291460 | tf_op jit(solution)/shard_map/broadcast_in_dim | solution.py:72
  21.5 3.1 %select_dynamic-update-slice_fusion = f32[2048,768]{1,0:T(8,128)} fusion(f32[2048,768]{1,0:T(8,128)} %broadcast_in_dim.69, s32[]{:T(128)S(6)} %select_n.414, f32[2048,1024]{1,0:T(8,128)} %param.4, pred[]{:T(512)S(6)} %lt.140), kind=kLoop, calls=%fused_computation.33 | loop fusion | flops 524288 | bytes 4194309 | tf_op jit(solution)/shard_map/dynamic_update_slice | solution.py:73
  24.8 0.7 collective-permute-start.12
  25.5 0.7 collective-permute-start.11
  26.2 1.3 collective-permute-start.10
  27.5 1.0 select_add_fusion.5
  28.6 0.7 collective-permute-start.8
  29.4 1.0 fusion.9
  30.4 0.7 collective-permute-start.7
  31.1 1.3 collective-permute-start.6
  32.4 1.3 iota_compare_fusion
  33.7 20.2 %collective-permute-done.6 = f32[256,256]{1,0:T(8,128)S(1)} collective-permute-done((f32[256,256]{1,0:T(8,128)S(1)}, f32[256,256]{1,0:T(8,128)S(1)}, u32[]{:S(2)}, u32[]{:S(2)}) %collective-permute-start.6) | collective-permute-done | bytes 262176 | tf_op jit(solution)/shard_map/ppermute | solution.py:57
  54.1 5.8 %collective-permute-done.10 = f32[256,768]{1,0:T(8,128)} collective-permute-done((f32[256,768]{1,0:T(8,128)S(1)}, f32[256,768]{1,0:T(8,128)}, u32[]{:S(2)}, u32[]{:S(2)}) %collective-permute-start.10) | collective-permute-done | bytes 786464 | tf_op jit(solution)/shard_map/ppermute | solution.py:47
  59.9 1.4 select_add_fusion.1
  61.2 1.3 collective-permute-start.15
  62.6 2.2 collective-permute-start.14
  64.8 2.3 collective-permute-start.13
  67.4 11.7 %cholesky.104 = f32[128,128]{1,0:T(8,128)S(1)} custom-call(f32[128,128]{1,0:T(8,128)S(1)} %copy.4), custom_call_target="Cholesky" | custom-call | tf_op jit(solution)/shard_map/jit(cholesky)/cholesky | solution.py:94
  79.2 0.6 compare_reduce_fusion.5
  80.4 9.8 %custom-call.10 = f32[1,128,128]{1,2,0:T(8,128)S(1)} custom-call(f32[1,128,128]{2,1,0:T(8,128)S(1)} %get-tuple-element.14), custom_call_target="InvertDiagBlocksLowerTriangular" | custom-call | tf_op jit(solution)/shard_map/jit(_solve_triangular)/triangular_solve | solution.py:95
  91.4 11.7 %cholesky.115 = f32[128,128]{1,0:T(8,128)S(1)} custom-call(f32[128,128]{1,0:T(8,128)S(1)} %copy.6), custom_call_target="Cholesky" | custom-call | tf_op jit(solution)/shard_map/jit(cholesky)/cholesky | solution.py:97
  103.1 0.6 compare_reduce_fusion.4
  104.4 10.2 %custom-call.11 = f32[1,128,128]{1,2,0:T(8,128)S(1)} custom-call(f32[1,128,128]{2,1,0:T(8,128)S(1)} %get-tuple-element.12), custom_call_target="InvertDiagBlocksLowerTriangular" | custom-call | tf_op jit(solution)/shard_map/jit(_solve_triangular)/triangular_solve | solution.py:98
  115.2 0.7 select_maximum_fusion
  116.6 4.0 %fusion.14 = f32[1024,256]{1,0:T(8,128)} fusion(f32[768,1024]{1,0:T(8,128)} %all-reduce.13.cloned.1.call-done, f32[128,128]{1,0:T(8,128)S(1)} %fusion.55, f32[128,128]{1,0:T(8,128)S(1)} %copy.8, f32[128,128]{1,0:T(8,128)S(1)} %convolution_negate_fusion.5), kind=kOutput, calls=%fused_computation.41 | convolution fusion | flops 805568512 | bytes 2293760 | tf_op jit(solution)/shard_map/dot_general | solution.py:147
  120.7 1.3 broadcast_select_fusion.1
  123.2 11.7 %cholesky.126 = f32[128,128]{1,0:T(8,128)S(1)} custom-call(f32[128,128]{1,0:T(8,128)S(1)} %copy.10), custom_call_target="Cholesky" | custom-call | tf_op jit(solution)/shard_map/jit(cholesky)/cholesky | solution.py:94
  135.6 0.7 select_bitcast_fusion.3
  136.3 9.8 %custom-call.12 = f32[1,128,128]{1,2,0:T(8,128)S(1)} custom-call(f32[1,128,128]{2,1,0:T(8,128)S(1)} %get-tuple-element.10), custom_call_target="InvertDiagBlocksLowerTriangular" | custom-call | tf_op jit(solution)/shard_map/jit(_solve_triangular)/triangular_solve | solution.py:95
  147.8 11.9 %cholesky.137 = f32[128,128]{1,0:T(8,128)S(1)} custom-call(f32[128,128]{1,0:T(8,128)S(1)} %copy.12), custom_call_target="Cholesky" | custom-call | tf_op jit(solution)/shard_map/jit(cholesky)/cholesky | solution.py:97
  159.8 0.6 compare_reduce_fusion.2
  160.4 1.3 select_bitcast_fusion.2
  161.7 9.8 %custom-call.13 = f32[1,128,128]{1,2,0:T(8,128)S(1)} custom-call(f32[1,128,128]{2,1,0:T(8,128)S(1)} %get-tuple-element.8), custom_call_target="InvertDiagBlocksLowerTriangular" | custom-call | tf_op jit(solution)/shard_map/jit(_solve_triangular)/triangular_solve | solution.py:98
  172.2 0.8 copy.29
  173.0 0.7 copy.28
  173.7 0.8 copy.31
  175.6 0.8 copy.32
  177.9 11.7 %cholesky.148 = f32[128,128]{1,0:T(8,128)S(1)} custom-call(f32[128,128]{1,0:T(8,128)S(1)} %copy.17), custom_call_target="Cholesky" | custom-call | tf_op jit(solution)/shard_map/jit(cholesky)/cholesky | solution.py:94
  190.3 1.3 select_bitcast_fusion.1
  191.6 10.0 %custom-call.14 = f32[1,128,128]{1,2,0:T(8,128)S(1)} custom-call(f32[1,128,128]{2,1,0:T(8,128)S(1)} %get-tuple-element.6), custom_call_target="InvertDiagBlocksLowerTriangular" | custom-call | tf_op jit(solution)/shard_map/jit(_solve_triangular)/triangular_solve | solution.py:95
  202.1 0.7 copy.30
  203.4 11.7 %cholesky.159 = f32[128,128]{1,0:T(8,128)S(1)} custom-call(f32[128,128]{1,0:T(8,128)S(1)} %copy.19), custom_call_target="Cholesky" | custom-call | tf_op jit(solution)/shard_map/jit(cholesky)/cholesky | solution.py:97
  215.8 1.3 select_bitcast_fusion
  217.0 9.8 %custom-call.15 = f32[1,128,128]{1,2,0:T(8,128)S(1)} custom-call(f32[1,128,128]{2,1,0:T(8,128)S(1)} %get-tuple-element.4), custom_call_target="InvertDiagBlocksLowerTriangular" | custom-call | tf_op jit(solution)/shard_map/jit(_solve_triangular)/triangular_solve | solution.py:98
  227.2 1.6 pad_select_fusion
  232.6 0.8 convolution_negate_fusion.1
  233.4 4.5 %fusion.10 = f32[1024,256]{1,0:T(8,128)} fusion(f32[768,1024]{1,0:T(8,128)S(1)} %copy-done.2, f32[128,128]{1,0:T(8,128)S(1)} %copy.14, f32[128,128]{1,0:T(8,128)S(1)} %convolution_negate_fusion.4, f32[128,256]{1,0:T(8,128)S(1)} %concatenate.91, f32[256,256]{1,0:T(8,128)S(1)} %convolution_negate_fusion.2), kind=kOutput, calls=%fused_computation.29 | convolution fusion | flops 1611005952 | bytes 3670016 | tf_op jit(solution)/shard_map/dot_general | solution.py:147
  238.0 6.2 %fusion.37 = f32[1024,256]{1,0:T(8,128)} fusion(f32[768,1024]{1,0:T(8,128)S(1)} %copy-done.2, f32[128,128]{1,0:T(8,128)S(1)} %copy.21, f32[128,128]{1,0:T(8,128)S(1)} %convolution_negate_fusion.3, f32[128,256]{1,0:T(8,128)S(1)} %concatenate.95, f32[256,256]{1,0:T(8,128)S(1)} %convolution_negate_fusion, f32[256,256]{1,0:T(8,128)S(1)} %convolution_negate_fusion.1), kind=kOutput, calls=%fused_computation.79 | convolution fusion | flops 2416705536 | bytes 4980736 | tf_op jit(solution)/shard_map/dot_general | solution.py:147
  244.1 7.9 %fusion.38 = f32[2048,256]{1,0:T(8,128)S(1)} fusion(f32[2048,768]{1,0:T(8,128)} %all-reduce.11.cloned.1.call-done, f32[128,128]{1,0:T(8,128)S(1)} %copy.21, f32[128,128]{1,0:T(8,128)S(1)} %convolution_negate_fusion.3, f32[128,256]{1,0:T(8,128)S(1)} %concatenate.95, f32[256,256]{1,0:T(8,128)S(1)} %convolution_negate_fusion, ...), kind=kOutput, calls=%fused_computation.80 | convolution fusion | flops 4832624640 | bytes 9175040 | tf_op jit(solution)/shard_map/dot_general | solution.py:147
  252.1 3.7 %fusion = f32[2048,256]{1,0:T(8,128)S(1)} fusion(f32[2048,768]{1,0:T(8,128)S(1)} %copy-done, f32[128,128]{1,0:T(8,128)S(1)} %copy-done.12, f32[128,128]{1,0:T(8,128)S(1)} %copy-done.10, f32[128,256]{1,0:T(8,128)S(1)} %concatenate.91, f32[256,256]{1,0:T(8,128)S(1)} %convolution_negate_fusion.2), kind=kOutput, calls=%fused_computation.2 | convolution fusion | flops 3221618688 | bytes 6815744 | tf_op jit(solution)/shard_map/dot_general | solution.py:147
  255.8 3.2 %fusion.12 = f32[2048,256]{1,0:T(8,128)} fusion(f32[2048,768]{1,0:T(8,128)S(1)} %copy-done, f32[128,128]{1,0:T(8,128)S(1)} %fusion.55, f32[128,128]{1,0:T(8,128)S(1)} %copy.8, f32[128,128]{1,0:T(8,128)S(1)} %copy-done.8), kind=kOutput, calls=%fused_computation.31 | convolution fusion | flops 1610874880 | bytes 4390912 | tf_op jit(solution)/shard_map/dot_general | solution.py:147
  259.0 2.2 pad_maximum_fusion
  261.2 2.8 fusion.26
  264.0 23.3 %subtract_select_fusion = f32[2048,1024]{1,0:T(8,128)} fusion(f32[2048,1024]{1,0:T(8,128)S(1)} %bitcast.95, pred[1024]{0:T(1024)(128)(4,1)S(1)} %fusion.85, pred[2048]{0:T(1024)(128)(4,1)S(1)} %fusion.79, f32[2048,768]{1,0:T(8,128)S(1)} %fusion.26, f32[1024,256]{1,0:T(8,128)S(1)} %copy-done.5, f32[1024,256]{1,0:T(8,128)S(1)} %copy-done.4, ...), kind=kOutput, calls=%fused_computation | convolution fusion | flops 19335217152 | bytes 26217472 | tf_op jit(solution)/shard_map/dot_general | solution.py:174
  (134 shorter events, 17.8 us)
Async XLA Ops:
  7.2 109.5 %all-reduce.13.cloned.1.call-start = ((), (), s32[]{:S(2)}) async-start(), calls=%async_computation.1 | async-start | bytes 6291456 | tf_op jit(solution)/shard_map/psum | solution.py:83
  8.9 1.7 copy-start.3
  10.6 233.5 %all-reduce.11.cloned.1.call-start = ((), (), s32[]{:S(2)}) async-start(), calls=%async_computation | async-start | bytes 12582912 | tf_op jit(solution)/shard_map/psum | solution.py:74
  11.6 2.2 collective-permute-start.2
  12.3 1.5 collective-permute-start.1
  13.0 0.8 collective-permute-start
  15.0 11.2 %collective-permute-start.5 = (f32[256,256]{1,0:T(8,128)S(1)}, f32[256,256]{1,0:T(8,128)S(1)}, u32[]{:S(2)}, u32[]{:S(2)}) collective-permute-start(f32[256,256]{1,0:T(8,128)S(1)} %get-tuple-element.20), channel_id=1, source_target_pairs={{0,12},{1,13},{2,14},{3,15}} | collective-permute-start | bytes 786440 | tf_op jit(solution)/shard_map/ppermute | solution.py:47
  15.7 11.9 %collective-permute-start.4 = (f32[256,256]{1,0:T(8,128)S(1)}, f32[256,256]{1,0:T(8,128)}, u32[]{:S(2)}, u32[]{:S(2)}) collective-permute-start(f32[256,256]{1,0:T(8,128)S(1)} %get-tuple-element.20), channel_id=1, source_target_pairs={{0,8},{1,9},{2,10},{3,11}} | collective-permute-start | bytes 786440 | tf_op jit(solution)/shard_map/ppermute | solution.py:47
  17.0 10.5 %collective-permute-start.3 = (f32[256,256]{1,0:T(8,128)S(1)}, f32[256,256]{1,0:T(8,128)}, u32[]{:S(2)}, u32[]{:S(2)}) collective-permute-start(f32[256,256]{1,0:T(8,128)S(1)} %get-tuple-element.20), channel_id=1, source_target_pairs={{0,4},{1,5},{2,6},{3,7}} | collective-permute-start | bytes 786440 | tf_op jit(solution)/shard_map/ppermute | solution.py:47
  24.8 29.3 %collective-permute-start.12 = (f32[256,768]{1,0:T(8,128)S(1)}, f32[256,768]{1,0:T(8,128)S(1)}, u32[]{:S(2)}, u32[]{:S(2)}) collective-permute-start(f32[256,768]{1,0:T(8,128)S(1)} %fusion.18), channel_id=1, source_target_pairs={{16,28},{17,29},{18,30},{19,31},{32,44},{33,45},{34,46},{35,47}} | collective-permute-start | bytes 2359304 | tf_op jit(solution)/shard_map/ppermute | solution.py:47
  25.5 28.6 %collective-permute-start.11 = (f32[256,768]{1,0:T(8,128)S(1)}, f32[256,768]{1,0:T(8,128)S(1)}, u32[]{:S(2)}, u32[]{:S(2)}) collective-permute-start(f32[256,768]{1,0:T(8,128)S(1)} %fusion.18), channel_id=1, source_target_pairs={{16,24},{17,25},{18,26},{19,27},{32,40},{33,41},{34,42},{35,43}} | collective-permute-start | bytes 2359304 | tf_op jit(solution)/shard_map/ppermute | solution.py:47
  26.2 33.6 %collective-permute-start.10 = (f32[256,768]{1,0:T(8,128)S(1)}, f32[256,768]{1,0:T(8,128)}, u32[]{:S(2)}, u32[]{:S(2)}) collective-permute-start(f32[256,768]{1,0:T(8,128)S(1)} %fusion.18), channel_id=1, source_target_pairs={{16,20},{17,21},{18,22},{19,23},{32,36},{33,37},{34,38},{35,39}} | collective-permute-start | bytes 2359304 | tf_op jit(solution)/shard_map/ppermute | solution.py:47
  28.6 2.5 collective-permute-start.8
  30.4 3.3 %collective-permute-start.7 = (f32[256,256]{1,0:T(8,128)S(1)}, f32[256,256]{1,0:T(8,128)S(1)}, u32[]{:S(2)}, u32[]{:S(2)}) collective-permute-start(f32[256,256]{1,0:T(8,128)S(1)} %select_add_fusion.5), channel_id=1, source_target_pairs={{0,64},{1,65},{2,66},{3,67},{4,68},{5,69},{6,70},{7,71},{8,72},{9,... | collective-permute-start | bytes 786440 | tf_op jit(solution)/shard_map/ppermute | solution.py:57
  31.1 22.9 %collective-permute-start.6 = (f32[256,256]{1,0:T(8,128)S(1)}, f32[256,256]{1,0:T(8,128)S(1)}, u32[]{:S(2)}, u32[]{:S(2)}) collective-permute-start(f32[256,256]{1,0:T(8,128)S(1)} %select_add_fusion.5), channel_id=1, source_target_pairs={{0,32},{1,33},{2,34},{3,35},{4,36},{5,37},{6,38},{7,39},{8,40},{9,... | collective-permute-start | bytes 786440 | tf_op jit(solution)/shard_map/ppermute | solution.py:57
  54.0 13.1 %collective-permute-start.9 = (f32[256,256]{1,0:T(8,128)S(1)}, f32[256,256]{1,0:T(8,128)S(1)}, u32[]{:S(2)}, u32[]{:S(2)}) collective-permute-start(f32[256,256]{1,0:T(8,128)S(1)} %select_add_fusion.4), channel_id=1, source_target_pairs={{0,16},{1,17},{2,18},{3,19},{4,20},{5,21},{6,22},{7,23},{8,24},{9,... | collective-permute-start | bytes 786440 | tf_op jit(solution)/shard_map/ppermute | solution.py:61
  61.2 53.6 %collective-permute-start.15 = (f32[256,768]{1,0:T(8,128)S(1)}, f32[256,768]{1,0:T(8,128)S(1)}, u32[]{:S(2)}, u32[]{:S(2)}) collective-permute-start(f32[256,768]{1,0:T(8,128)S(1)} %select_add_fusion.1), channel_id=1, source_target_pairs={{16,112},{17,113},{18,114},{19,115},{20,116},{21,117},{22,118},{23... | collective-permute-start | bytes 2359304 | tf_op jit(solution)/shard_map/ppermute | solution.py:57
  62.6 52.2 %collective-permute-start.14 = (f32[256,768]{1,0:T(8,128)S(1)}, f32[256,768]{1,0:T(8,128)}, u32[]{:S(2)}, u32[]{:S(2)}) collective-permute-start(f32[256,768]{1,0:T(8,128)S(1)} %select_add_fusion.1), channel_id=1, source_target_pairs={{16,80},{17,81},{18,82},{19,83},{20,84},{21,85},{22,86},{23,87},{2... | collective-permute-start | bytes 2359304 | tf_op jit(solution)/shard_map/ppermute | solution.py:57
  64.8 50.1 %collective-permute-start.13 = (f32[256,768]{1,0:T(8,128)S(1)}, f32[256,768]{1,0:T(8,128)}, u32[]{:S(2)}, u32[]{:S(2)}) collective-permute-start(f32[256,768]{1,0:T(8,128)S(1)} %select_add_fusion.1), channel_id=1, source_target_pairs={{16,48},{17,49},{18,50},{19,51},{20,52},{21,53},{22,54},{23,55},{2... | collective-permute-start | bytes 2359304 | tf_op jit(solution)/shard_map/ppermute | solution.py:57
  115.1 5.6 %collective-permute-start.16 = (f32[256,768]{1,0:T(8,128)S(1)}, f32[256,768]{1,0:T(8,128)}, u32[]{:S(2)}, u32[]{:S(2)}) collective-permute-start(f32[256,768]{1,0:T(8,128)S(1)} %select_add_fusion), channel_id=1, source_target_pairs={{0,16},{1,17},{2,18},{3,19},{4,20},{5,21},{6,22},{7,23},{8,24},{9,... | collective-permute-start | bytes 2359304 | tf_op jit(solution)/shard_map/ppermute | solution.py:61
  116.6 114.0 %copy-start.7 = (f32[128,128]{1,0:T(8,128)}, f32[128,128]{1,0:T(8,128)S(1)}, u32[]{:S(2)}) copy-start(f32[128,128]{1,0:T(8,128)S(1)} %convolution_negate_fusion.5) | copy-start | bytes 196612
  172.0 61.3 %copy-start.9 = (f32[128,128]{1,0:T(8,128)}, f32[128,128]{1,0:T(8,128)S(1)}, u32[]{:S(2)}) copy-start(f32[128,128]{1,0:T(8,128)S(1)} %convolution_negate_fusion.4) | copy-start | bytes 196612
  172.2 61.2 %copy-start.11 = (f32[128,128]{1,0:T(8,128)}, f32[128,128]{1,0:T(8,128)S(1)}, u32[]{:S(2)}) copy-start(f32[128,128]{1,0:T(8,128)S(1)} %copy.14) | copy-start | bytes 196612
  228.8 4.6 %copy-start.2 = (f32[768,1024]{1,0:T(8,128)S(1)}, f32[768,1024]{1,0:T(8,128)}, u32[]{:S(2)}) copy-start(f32[768,1024]{1,0:T(8,128)} %all-reduce.13.cloned.1.call-done) | copy-start | bytes 9437188
  244.1 7.9 %copy-start = (f32[2048,768]{1,0:T(8,128)S(1)}, f32[2048,768]{1,0:T(8,128)}, u32[]{:S(2)}) copy-start(f32[2048,768]{1,0:T(8,128)} %all-reduce.11.cloned.1.call-done) | copy-start | bytes 18874372
  244.1 7.9 %copy-start.10 = (f32[128,128]{1,0:T(8,128)S(1)}, f32[128,128]{1,0:T(8,128)}, u32[]{:S(2)}) copy-start(f32[128,128]{1,0:T(8,128)} %copy-done.9) | copy-start | bytes 196612
  244.1 7.9 %copy-start.12 = (f32[128,128]{1,0:T(8,128)S(1)}, f32[128,128]{1,0:T(8,128)}, u32[]{:S(2)}) copy-start(f32[128,128]{1,0:T(8,128)} %copy-done.11) | copy-start | bytes 196612
  252.1 3.7 %copy-start.8 = (f32[128,128]{1,0:T(8,128)S(1)}, f32[128,128]{1,0:T(8,128)}, u32[]{:S(2)}) copy-start(f32[128,128]{1,0:T(8,128)} %copy-done.7) | copy-start | bytes 196612
  255.8 8.2 %slice-start = ((s8[8388608]{0:T(1024)(128)(4,1)}), s8[4194304]{0:T(1024)(128)(4,1)S(1)}, s32[]{:S(2)}) async-start(s8[8388608]{0:T(1024)(128)(4,1)} %bitcast.94), calls=%async_computation.2 | async-start | bytes 8388608
  258.9 2.2 copy-start.13
  259.0 2.2 copy-start.14
  259.0 5.0 %slice-start.1 = ((s8[8388608]{0:T(1024)(128)(4,1)}), s8[4194304]{0:T(1024)(128)(4,1)S(1)}, s32[]{:S(2)}) async-start(s8[8388608]{0:T(1024)(128)(4,1)} %bitcast.94), calls=%async_computation.3 | async-start | bytes 8388608
  261.1 2.9 copy-start.4
  261.1 2.9 copy-start.5
  261.1 2.9 copy-start.6
  264.0 23.3 %copy-start.1 = (f32[2048,768]{1,0:T(8,128)}, f32[2048,768]{1,0:T(8,128)S(1)}, u32[]{:S(2)}) copy-start(f32[2048,768]{1,0:T(8,128)S(1)} %fusion.26) | copy-start | bytes 18874372
Sparse Core Ops, SparseCore 0:
  10.9 78.8 all-reduce.12
  93.8 126.4 all-reduce.10
where the time goes:
time: 300 us; the launch traced here: 294 us
  other arithmetic  159 us (53%)
  matrix products  65.4 us (22%)
  waiting for transfers between devices  26.1 us (9%)
  starting transfers between devices  16.9 us (6%)
  between operations  15.6 us (5%)
  local copies, waits for them, and re-layouts  11.6 us (4%)
    another operation x9, other arithmetic, factor_block(): bottom = jnp.linalg.cholesky(schur[half:, half:] - mul(side, side, True))  37.3 us
    another operation x9, other arithmetic, factor_block(): top = jnp.linalg.cholesky(schur[:half, :half])  37.2 us
    another operation x6, other arithmetic, factor_block(): bottom_inv = jax.scipy.linalg.solve_triangular(bottom, eye, lower=True)  32.9 us
    another operation x6, other arithmetic, factor_block(): top_inv = jax.scipy.linalg.solve_triangular(top, eye, lower=True)  32.1 us
    dot_general x6, matrix products, apply_inverse(): lax.dot_general(piece, inverse[j * BLOCK:hi, :hi], (((axis,), (1,)), ((),...  29.5 us
    dot_general x1, matrix products, shards(): lax.dot_general(panels, across, (((1,), (1,)), ((), ())), precision=lax.P...  23.3 us
    ppermute x6, waiting for transfers between devices, gather_corner(): got = lax.ppermute(mine, ('row', 'col'), pairs)  20.3 us
    dot_general x26, matrix products, mul(): lax.dot_general(a, b, dims, precision=lax.Precision.HIGHEST, preferred_el...  10.9 us
  transfers between devices with their start and end apart: 19, of which 2 were waited for; matrix products, arithmetic and copies ran while one was open for 64% of the time, Pallas kernels for 0%

commit v1 on v0

--- a/solution.py
+++ b/solution.py
@@ -169,8 +169,9 @@
     panels = apply_inverse(band_cols, inverse, 1)
     across = apply_inverse(band_rows, inverse, 0)
     own = lax.dynamic_slice_in_dim(factor, jnp.minimum(row_index, STEPS - 1) * BLOCK, BLOCK, 0)
-    head = jnp.where(row_index < STEPS, own, panels[:BLOCK])
-    panels = lax.dynamic_update_slice(panels, head, (0, 0))
+    own = jnp.pad(own, ((0, rows_local - BLOCK), (0, 0)))
+    head = (jnp.arange(rows_local) < BLOCK)[:, None] & (row_index < STEPS)
+    panels = jnp.where(head, own, panels)
     update = lax.dot_general(
         panels, across, (((1,), (1,)), ((), ())),
         precision=lax.Precision.HIGHEST, preferred_element_type=jnp.float32,

time: 300 us -> 294 us (0.980)
  other arithmetic: 159 us -> 155 us
  matrix products: 65.4 us -> 62 us
    dot_general x6, matrix products: 29.5 us -> 26.3 us  [apply_inverse(): lax.dot_general(piece, inverse[j * BLOCK:hi, :hi], (((axis,), (1,)), ((),...]
  transfers between devices with their start and end apart: 19 -> 19, of which waited for: 2 -> 2; matrix products, arithmetic and copies ran while one was open for 64% -> 65% of each run, Pallas kernels for 0% -> 0%
where the time goes in v1:
time: 294 us; the launch traced here: 289 us
  other arithmetic  155 us (53%)
  matrix products  62 us (21%)
  waiting for transfers between devices  26.9 us (9%)
  starting transfers between devices  16.3 us (6%)
  between operations  15.6 us (5%)
  local copies, waits for them, and re-layouts  12.7 us (4%)
    another operation x9, other arithmetic, factor_block(): bottom = jnp.linalg.cholesky(schur[half:, half:] - mul(side, side, True))  37.4 us
    another operation x9, other arithmetic, factor_block(): top = jnp.linalg.cholesky(schur[:half, :half])  37.2 us
    another operation x6, other arithmetic, factor_block(): top_inv = jax.scipy.linalg.solve_triangular(top, eye, lower=True)  32.1 us
    another operation x6, other arithmetic, factor_block(): bottom_inv = jax.scipy.linalg.solve_triangular(bottom, eye, lower=True)  31.7 us
    dot_general x6, matrix products, apply_inverse(): lax.dot_general(piece, inverse[j * BLOCK:hi, :hi], (((axis,), (1,)), ((),...  26.3 us
    dot_general x1, matrix products, shards(): lax.dot_general(panels, across, (((1,), (1,)), ((), ())), precision=lax.P...  23.2 us
    ppermute x6, waiting for transfers between devices, gather_corner(): got = lax.ppermute(mine, ('row', 'col'), pairs)  22.2 us
    dot_general x26, matrix products, mul(): lax.dot_general(a, b, dims, precision=lax.Precision.HIGHEST, preferred_el...  10.9 us
  transfers between devices with their start and end apart: 19, of which 2 were waited for; matrix products, arithmetic and copies ran while one was open for 65% of the time, Pallas kernels for 0%

profile of v1, /device:TPU:10, one launch (start us, length us, event | category | flops | bytes accessed | tf_op | source)
XLA Modules:
  0.0 288.6 jit_solution(459818413419890631)
XLA Ops:
  7.6 1.3 select_dynamic-update-slice_fusion.1
  8.9 1.7 copy-done.3
  10.7 1.0 slice.75
  11.6 0.7 collective-permute-start.2
  12.3 0.7 collective-permute-start.1
  13.0 0.7 collective-permute-start
  13.8 1.1 select_add_fusion.2
  15.0 0.7 collective-permute-start.5
  15.7 0.7 collective-permute-start.4
  16.3 0.7 collective-permute-start.3
  17.0 3.1 %broadcast_in_dim.81 = f32[2048,768]{1,0:T(8,128)} broadcast(f32[]{:T(128)} %constant.252.clone.1), dimensions={} | broadcast | bytes 6291460 | tf_op jit(solution)/shard_map/broadcast_in_dim | solution.py:72
  20.1 3.2 %select_dynamic-update-slice_fusion = f32[2048,768]{1,0:T(8,128)} fusion(f32[2048,768]{1,0:T(8,128)} %broadcast_in_dim.81, s32[]{:T(128)S(6)} %select_n.491, f32[2048,1024]{1,0:T(8,128)} %param.4, pred[]{:T(512)S(6)} %lt.164), kind=kLoop, calls=%fused_computation.33 | loop fusion | flops 524288 | bytes 4194309 | tf_op jit(solution)/shard_map/dynamic_update_slice | solution.py:73
  23.6 0.7 collective-permute-start.12
  24.3 1.5 collective-permute-start.11
  25.8 1.3 collective-permute-start.10
  27.2 0.7 collective-permute-start.8
  28.2 0.7 collective-permute-start.7
  28.9 1.3 collective-permute-start.6
  30.2 1.4 iota_compare_fusion
  31.5 22.2 %collective-permute-done.6 = f32[256,256]{1,0:T(8,128)S(1)} collective-permute-done((f32[256,256]{1,0:T(8,128)S(1)}, f32[256,256]{1,0:T(8,128)S(1)}, u32[]{:S(2)}, u32[]{:S(2)}) %collective-permute-start.6) | collective-permute-done | bytes 262176 | tf_op jit(solution)/shard_map/ppermute | solution.py:57
  53.9 4.7 %collective-permute-done.10 = f32[256,768]{1,0:T(8,128)} collective-permute-done((f32[256,768]{1,0:T(8,128)S(1)}, f32[256,768]{1,0:T(8,128)}, u32[]{:S(2)}, u32[]{:S(2)}) %collective-permute-start.10) | collective-permute-done | bytes 786464 | tf_op jit(solution)/shard_map/ppermute | solution.py:47
  58.5 1.4 select_add_fusion.1
  59.9 1.3 collective-permute-start.15
  61.3 2.2 collective-permute-start.14
  63.4 2.3 collective-permute-start.13
  66.1 11.7 %cholesky.104 = f32[128,128]{1,0:T(8,128)S(1)} custom-call(f32[128,128]{1,0:T(8,128)S(1)} %copy.4), custom_call_target="Cholesky" | custom-call | tf_op jit(solution)/shard_map/jit(cholesky)/cholesky | solution.py:94
  79.0 9.8 %custom-call.10 = f32[1,128,128]{1,2,0:T(8,128)S(1)} custom-call(f32[1,128,128]{2,1,0:T(8,128)S(1)} %get-tuple-element.14), custom_call_target="InvertDiagBlocksLowerTriangular" | custom-call | tf_op jit(solution)/shard_map/jit(_solve_triangular)/triangular_solve | solution.py:95
  90.0 11.7 %cholesky.115 = f32[128,128]{1,0:T(8,128)S(1)} custom-call(f32[128,128]{1,0:T(8,128)S(1)} %copy.6), custom_call_target="Cholesky" | custom-call | tf_op jit(solution)/shard_map/jit(cholesky)/cholesky | solution.py:97
  103.0 10.2 %custom-call.11 = f32[1,128,128]{1,2,0:T(8,128)S(1)} custom-call(f32[1,128,128]{2,1,0:T(8,128)S(1)} %get-tuple-element.12), custom_call_target="InvertDiagBlocksLowerTriangular" | custom-call | tf_op jit(solution)/shard_map/jit(_solve_triangular)/triangular_solve | solution.py:98
  113.5 0.9 copy-done.10
  114.6 0.7 select_maximum_fusion.1
  116.1 4.0 %fusion.14 = f32[1024,256]{1,0:T(8,128)} fusion(f32[768,1024]{1,0:T(8,128)} %all-reduce.14.cloned.1.call-done, f32[128,128]{1,0:T(8,128)S(1)} %fusion.53, f32[128,128]{1,0:T(8,128)S(1)} %copy.9, f32[128,128]{1,0:T(8,128)S(1)} %convolution_negate_fusion.5), kind=kOutput, calls=%fused_computation.41 | convolution fusion | flops 805568512 | bytes 2293760 | tf_op jit(solution)/shard_map/dot_general | solution.py:147
  120.1 1.2 broadcast_select_fusion.1
  122.6 11.7 %cholesky.126 = f32[128,128]{1,0:T(8,128)S(1)} custom-call(f32[128,128]{1,0:T(8,128)S(1)} %copy.11), custom_call_target="Cholesky" | custom-call | tf_op jit(solution)/shard_map/jit(cholesky)/cholesky | solution.py:94
  134.3 0.7 compare_reduce_fusion.3
  135.0 1.3 select_bitcast_fusion.3
  136.3 9.8 %custom-call.12 = f32[1,128,128]{1,2,0:T(8,128)S(1)} custom-call(f32[1,128,128]{2,1,0:T(8,128)S(1)} %get-tuple-element.10), custom_call_target="InvertDiagBlocksLowerTriangular" | custom-call | tf_op jit(solution)/shard_map/jit(_solve_triangular)/triangular_solve | solution.py:95
  148.4 11.9 %cholesky.137 = f32[128,128]{1,0:T(8,128)S(1)} custom-call(f32[128,128]{1,0:T(8,128)S(1)} %copy.13), custom_call_target="Cholesky" | custom-call | tf_op jit(solution)/shard_map/jit(cholesky)/cholesky | solution.py:97
  160.3 0.7 compare_reduce_fusion.2
  161.0 0.6 select_bitcast_fusion.2
  161.7 9.8 %custom-call.13 = f32[1,128,128]{1,2,0:T(8,128)S(1)} custom-call(f32[1,128,128]{2,1,0:T(8,128)S(1)} %get-tuple-element.8), custom_call_target="InvertDiagBlocksLowerTriangular" | custom-call | tf_op jit(solution)/shard_map/jit(_solve_triangular)/triangular_solve | solution.py:98
  172.2 0.8 copy.15
  173.1 0.8 copy.23
  174.3 0.8 copy.24
  176.6 11.7 %cholesky.148 = f32[128,128]{1,0:T(8,128)S(1)} custom-call(f32[128,128]{1,0:T(8,128)S(1)} %copy.19), custom_call_target="Cholesky" | custom-call | tf_op jit(solution)/shard_map/jit(cholesky)/cholesky | solution.py:94
  188.4 0.7 compare_reduce_fusion.1
  189.0 0.6 select_bitcast_fusion.1
  189.7 10.0 %custom-call.14 = f32[1,128,128]{1,2,0:T(8,128)S(1)} custom-call(f32[1,128,128]{2,1,0:T(8,128)S(1)} %get-tuple-element.6), custom_call_target="InvertDiagBlocksLowerTriangular" | custom-call | tf_op jit(solution)/shard_map/jit(_solve_triangular)/triangular_solve | solution.py:95
  200.3 0.7 copy.22
  201.5 11.7 %cholesky.159 = f32[128,128]{1,0:T(8,128)S(1)} custom-call(f32[128,128]{1,0:T(8,128)S(1)} %copy.21), custom_call_target="Cholesky" | custom-call | tf_op jit(solution)/shard_map/jit(cholesky)/cholesky | solution.py:97
  213.2 0.7 compare_reduce_fusion
  213.9 0.6 select_bitcast_fusion
  214.6 9.8 %custom-call.15 = f32[1,128,128]{1,2,0:T(8,128)S(1)} custom-call(f32[1,128,128]{2,1,0:T(8,128)S(1)} %get-tuple-element.4), custom_call_target="InvertDiagBlocksLowerTriangular" | custom-call | tf_op jit(solution)/shard_map/jit(_solve_triangular)/triangular_solve | solution.py:98
  224.7 1.0 pad_select_fusion
  225.8 3.1 %fusion.24 = f32[256,768]{1,0:T(8,128)} fusion(s32[]{:T(128)S(6)} %select_n.488, f32[256,256]{1,0:T(8,128)S(1)} %copy-done.8, f32[128,128]{1,0:T(8,128)S(1)} %copy.14, f32[128,128]{1,0:T(8,128)S(1)} %get-tuple-element.9, f32[256,256]{1,0:T(8,128)S(1)} %broadcast_in_dim.79, f32[256,256]{1,0:T(8,128)S(1)} %copy-done.9, f32[256,256]{1,0:T(8,128)} %copy.24, ...), kind=kLoop, calls=%fused_computation.55 | loop fusion | flops 3735552 | bytes 3802112 | tf_op jit(solution)/shard_map/concatenate | solution.py:133
  231.3 0.8 convolution_negate_fusion.2
  233.5 3.5 %fusion.10 = f32[1024,256]{1,0:T(8,128)S(1)} fusion(f32[768,1024]{1,0:T(8,128)S(1)} %copy-done.2, f32[128,128]{1,0:T(8,128)S(1)} %copy.17, f32[128,128]{1,0:T(8,128)S(1)} %convolution_negate_fusion.4, f32[128,256]{1,0:T(8,128)S(1)} %concatenate.99, f32[256,256]{1,0:T(8,128)S(1)} %convolution_negate_fusion.2), kind=kOutput, calls=%fused_computation.29 | convolution fusion | flops 1611005952 | bytes 3670016 | tf_op jit(solution)/shard_map/dot_general | solution.py:147
  237.1 5.2 %fusion.35 = f32[1024,256]{1,0:T(8,128)S(1)} fusion(f32[768,1024]{1,0:T(8,128)S(1)} %copy-done.2, f32[128,128]{1,0:T(8,128)S(1)} %copy.27, f32[128,128]{1,0:T(8,128)S(1)} %convolution_negate_fusion.3, f32[128,256]{1,0:T(8,128)S(1)} %concatenate.108, f32[256,256]{1,0:T(8,128)S(1)} %convolution_negate_fusion, f32[256,256]{1,0:T(8,128)S(1)} %convolution_negate_fusion.1), kind=kOutput, calls=%fused_computation.77 | convolution fusion | flops 2416705536 | bytes 4980736 | tf_op jit(solution)/shard_map/dot_general | solution.py:147
  242.3 7.9 %fusion.36 = f32[2048,256]{1,0:T(8,128)S(1)} fusion(f32[2048,768]{1,0:T(8,128)} %all-reduce.12.cloned.1.call-done, f32[128,128]{1,0:T(8,128)S(1)} %copy.27, f32[128,128]{1,0:T(8,128)} %copy-done.6, f32[128,256]{1,0:T(8,128)S(1)} %concatenate.108, f32[256,256]{1,0:T(8,128)S(1)} %convolution_negate_fusion, f32[256,256]{1,0:T(8,128)S(1)} %convolution_negate_fusion.1), kind=kOutput, calls=%fused_computation.78 | convolution fusion | flops 4832624640 | bytes 9175040 | tf_op jit(solution)/shard_map/dot_general | solution.py:147
  250.2 3.7 %fusion = f32[2048,256]{1,0:T(8,128)S(1)} fusion(f32[2048,768]{1,0:T(8,128)S(1)} %copy-done, f32[128,128]{1,0:T(8,128)S(1)} %copy.17, f32[128,128]{1,0:T(8,128)S(1)} %convolution_negate_fusion.4, f32[128,256]{1,0:T(8,128)S(1)} %concatenate.99, f32[256,256]{1,0:T(8,128)S(1)} %convolution_negate_fusion.2), kind=kOutput, calls=%fused_computation.2 | convolution fusion | flops 3221618688 | bytes 6815744 | tf_op jit(solution)/shard_map/dot_general | solution.py:147
  253.9 1.9 fusion.12
  255.9 1.5 maximum_select_fusion
  257.5 0.7 slice-done.1
  258.4 23.2 %subtract_select_fusion = f32[2048,1024]{1,0:T(8,128)} fusion(f32[2048,1024]{1,0:T(8,128)S(1)} %bitcast.95, pred[1024]{0:T(1024)(128)(4,1)S(1)} %fusion.83, pred[2048]{0:T(1024)(128)(4,1)S(1)} %fusion.76, f32[2048,768]{1,0:T(8,128)S(1)} %maximum_select_fusion, f32[1024,256]{1,0:T(8,128)S(1)} %fusion.35, f32[1024,256]{1,0:T(8,128)S(1)} %fusion.10, ...), kind=kOutput, calls=%fused_computation | convolution fusion | flops 19335217152 | bytes 26217472 | tf_op jit(solution)/shard_map/dot_general | solution.py:175
  (127 shorter events, 17.7 us)
Async XLA Ops:
  7.2 108.9 %all-reduce.14.cloned.1.call-start = ((), (), s32[]{:S(2)}) async-start(), calls=%async_computation.1 | async-start | bytes 6291456 | tf_op jit(solution)/shard_map/psum | solution.py:83
  8.9 1.7 copy-start.3
  10.6 231.7 %all-reduce.12.cloned.1.call-start = ((), (), s32[]{:S(2)}) async-start(), calls=%async_computation | async-start | bytes 12582912 | tf_op jit(solution)/shard_map/psum | solution.py:74
  11.6 2.2 collective-permute-start.2
  12.3 1.5 collective-permute-start.1
  13.0 0.8 collective-permute-start
  15.0 10.9 %collective-permute-start.5 = (f32[256,256]{1,0:T(8,128)S(1)}, f32[256,256]{1,0:T(8,128)S(1)}, u32[]{:S(2)}, u32[]{:S(2)}) collective-permute-start(f32[256,256]{1,0:T(8,128)S(1)} %get-tuple-element.20), channel_id=1, source_target_pairs={{0,12},{1,13},{2,14},{3,15}} | collective-permute-start | bytes 786440 | tf_op jit(solution)/shard_map/ppermute | solution.py:47
  15.7 11.5 %collective-permute-start.4 = (f32[256,256]{1,0:T(8,128)S(1)}, f32[256,256]{1,0:T(8,128)S(1)}, u32[]{:S(2)}, u32[]{:S(2)}) collective-permute-start(f32[256,256]{1,0:T(8,128)S(1)} %get-tuple-element.20), channel_id=1, source_target_pairs={{0,8},{1,9},{2,10},{3,11}} | collective-permute-start | bytes 786440 | tf_op jit(solution)/shard_map/ppermute | solution.py:47
  16.3 10.8 %collective-permute-start.3 = (f32[256,256]{1,0:T(8,128)S(1)}, f32[256,256]{1,0:T(8,128)S(1)}, u32[]{:S(2)}, u32[]{:S(2)}) collective-permute-start(f32[256,256]{1,0:T(8,128)S(1)} %get-tuple-element.20), channel_id=1, source_target_pairs={{0,4},{1,5},{2,6},{3,7}} | collective-permute-start | bytes 786440 | tf_op jit(solution)/shard_map/ppermute | solution.py:47
  23.6 30.3 %collective-permute-start.12 = (f32[256,768]{1,0:T(8,128)S(1)}, f32[256,768]{1,0:T(8,128)S(1)}, u32[]{:S(2)}, u32[]{:S(2)}) collective-permute-start(f32[256,768]{1,0:T(8,128)S(1)} %fusion.18), channel_id=1, source_target_pairs={{16,28},{17,29},{18,30},{19,31},{32,44},{33,45},{34,46},{35,47}} | collective-permute-start | bytes 2359304 | tf_op jit(solution)/shard_map/ppermute | solution.py:47
  24.3 29.6 %collective-permute-start.11 = (f32[256,768]{1,0:T(8,128)S(1)}, f32[256,768]{1,0:T(8,128)}, u32[]{:S(2)}, u32[]{:S(2)}) collective-permute-start(f32[256,768]{1,0:T(8,128)S(1)} %fusion.18), channel_id=1, source_target_pairs={{16,24},{17,25},{18,26},{19,27},{32,40},{33,41},{34,42},{35,43}} | collective-permute-start | bytes 2359304 | tf_op jit(solution)/shard_map/ppermute | solution.py:47
  25.8 32.7 %collective-permute-start.10 = (f32[256,768]{1,0:T(8,128)S(1)}, f32[256,768]{1,0:T(8,128)}, u32[]{:S(2)}, u32[]{:S(2)}) collective-permute-start(f32[256,768]{1,0:T(8,128)S(1)} %fusion.18), channel_id=1, source_target_pairs={{16,20},{17,21},{18,22},{19,23},{32,36},{33,37},{34,38},{35,39}} | collective-permute-start | bytes 2359304 | tf_op jit(solution)/shard_map/ppermute | solution.py:47
  27.2 1.6 collective-permute-start.8
  28.2 3.4 %collective-permute-start.7 = (f32[256,256]{1,0:T(8,128)S(1)}, f32[256,256]{1,0:T(8,128)S(1)}, u32[]{:S(2)}, u32[]{:S(2)}) collective-permute-start(f32[256,256]{1,0:T(8,128)S(1)} %select_add_fusion.5), channel_id=1, source_target_pairs={{0,64},{1,65},{2,66},{3,67},{4,68},{5,69},{6,70},{7,71},{8,72},{9,... | collective-permute-start | bytes 786440 | tf_op jit(solution)/shard_map/ppermute | solution.py:57
  28.9 24.8 %collective-permute-start.6 = (f32[256,256]{1,0:T(8,128)S(1)}, f32[256,256]{1,0:T(8,128)S(1)}, u32[]{:S(2)}, u32[]{:S(2)}) collective-permute-start(f32[256,256]{1,0:T(8,128)S(1)} %select_add_fusion.5), channel_id=1, source_target_pairs={{0,32},{1,33},{2,34},{3,35},{4,36},{5,37},{6,38},{7,39},{8,40},{9,... | collective-permute-start | bytes 786440 | tf_op jit(solution)/shard_map/ppermute | solution.py:57
  53.8 12.0 %collective-permute-start.9 = (f32[256,256]{1,0:T(8,128)S(1)}, f32[256,256]{1,0:T(8,128)S(1)}, u32[]{:S(2)}, u32[]{:S(2)}) collective-permute-start(f32[256,256]{1,0:T(8,128)S(1)} %select_add_fusion.4), channel_id=1, source_target_pairs={{0,16},{1,17},{2,18},{3,19},{4,20},{5,21},{6,22},{7,23},{8,24},{9,... | collective-permute-start | bytes 786440 | tf_op jit(solution)/shard_map/ppermute | solution.py:61
  59.9 53.5 %collective-permute-start.15 = (f32[256,768]{1,0:T(8,128)S(1)}, f32[256,768]{1,0:T(8,128)S(1)}, u32[]{:S(2)}, u32[]{:S(2)}) collective-permute-start(f32[256,768]{1,0:T(8,128)S(1)} %select_add_fusion.1), channel_id=1, source_target_pairs={{16,112},{17,113},{18,114},{19,115},{20,116},{21,117},{22,118},{23... | collective-permute-start | bytes 2359304 | tf_op jit(solution)/shard_map/ppermute | solution.py:57
  61.3 52.2 %collective-permute-start.14 = (f32[256,768]{1,0:T(8,128)S(1)}, f32[256,768]{1,0:T(8,128)}, u32[]{:S(2)}, u32[]{:S(2)}) collective-permute-start(f32[256,768]{1,0:T(8,128)S(1)} %select_add_fusion.1), channel_id=1, source_target_pairs={{16,80},{17,81},{18,82},{19,83},{20,84},{21,85},{22,86},{23,87},{2... | collective-permute-start | bytes 2359304 | tf_op jit(solution)/shard_map/ppermute | solution.py:57
  63.4 50.9 %collective-permute-start.13 = (f32[256,768]{1,0:T(8,128)S(1)}, f32[256,768]{1,0:T(8,128)}, u32[]{:S(2)}, u32[]{:S(2)}) collective-permute-start(f32[256,768]{1,0:T(8,128)S(1)} %select_add_fusion.1), channel_id=1, source_target_pairs={{16,48},{17,49},{18,50},{19,51},{20,52},{21,53},{22,54},{23,55},{2... | collective-permute-start | bytes 2359304 | tf_op jit(solution)/shard_map/ppermute | solution.py:57
  113.5 0.9 copy-start.10
  114.6 5.5 %collective-permute-start.16 = (f32[256,768]{1,0:T(8,128)S(1)}, f32[256,768]{1,0:T(8,128)}, u32[]{:S(2)}, u32[]{:S(2)}) collective-permute-start(f32[256,768]{1,0:T(8,128)S(1)} %select_add_fusion), channel_id=1, source_target_pairs={{0,16},{1,17},{2,18},{3,19},{4,20},{5,21},{6,22},{7,23},{8,24},{9,... | collective-permute-start | bytes 2359304 | tf_op jit(solution)/shard_map/ppermute | solution.py:61
  175.8 50.0 %copy-start.7 = (f32[256,256]{1,0:T(8,128)S(1)}, f32[256,256]{1,0:T(8,128)}, u32[]{:S(2)}) copy-start(f32[256,256]{1,0:T(8,128)} %select_maximum_fusion.1) | copy-start | bytes 786436
  176.4 49.4 %copy-start.8 = (f32[256,256]{1,0:T(8,128)S(1)}, f32[256,256]{1,0:T(8,128)}, u32[]{:S(2)}) copy-start(f32[256,256]{1,0:T(8,128)} %copy.15) | copy-start | bytes 786436
  176.4 49.4 %copy-start.9 = (f32[256,256]{1,0:T(8,128)S(1)}, f32[256,256]{1,0:T(8,128)}, u32[]{:S(2)}) copy-start(f32[256,256]{1,0:T(8,128)} %copy.23) | copy-start | bytes 786436
  228.9 4.6 %copy-start.2 = (f32[768,1024]{1,0:T(8,128)S(1)}, f32[768,1024]{1,0:T(8,128)}, u32[]{:S(2)}) copy-start(f32[768,1024]{1,0:T(8,128)} %all-reduce.14.cloned.1.call-done) | copy-start | bytes 9437188
  229.5 7.5 %copy-start.6 = (f32[128,128]{1,0:T(8,128)}, f32[128,128]{1,0:T(8,128)S(1)}, u32[]{:S(2)}) copy-start(f32[128,128]{1,0:T(8,128)S(1)} %convolution_negate_fusion.3) | copy-start | bytes 196612
  242.3 7.9 %copy-start = (f32[2048,768]{1,0:T(8,128)S(1)}, f32[2048,768]{1,0:T(8,128)}, u32[]{:S(2)}) copy-start(f32[2048,768]{1,0:T(8,128)} %all-reduce.12.cloned.1.call-done) | copy-start | bytes 18874372
  250.2 5.7 %copy-start.5 = (f32[256,768]{1,0:T(8,128)S(1)}, f32[256,768]{1,0:T(8,128)}, u32[]{:S(2)}) copy-start(f32[256,768]{1,0:T(8,128)} %fusion.24) | copy-start | bytes 2359300
  253.9 3.5 %slice-start = ((s8[8388608]{0:T(1024)(128)(4,1)}), s8[4194304]{0:T(1024)(128)(4,1)S(1)}, s32[]{:S(2)}) async-start(s8[8388608]{0:T(1024)(128)(4,1)} %bitcast.94), calls=%async_computation.2 | async-start | bytes 8388608
  255.9 2.3 slice-start.1
  255.9 2.5 copy-start.4
  258.4 23.2 %copy-start.1 = (f32[2048,768]{1,0:T(8,128)}, f32[2048,768]{1,0:T(8,128)S(1)}, u32[]{:S(2)}) copy-start(f32[2048,768]{1,0:T(8,128)S(1)} %maximum_select_fusion) | copy-start | bytes 18874372
Sparse Core Ops, SparseCore 0:
  10.9 78.9 all-reduce.13
  94.0 125.0 all-reduce.11

commit v2 on v1

--- a/solution.py
+++ b/solution.py
@@ -57,7 +57,8 @@
             got = lax.ppermute(mine, ("row", "col"), pairs)
             source = 0 if len(group) == 1 else 2 - row_index % 2
             held = held + jnp.where((row_index - 2 * shift) % row_count == source, got, jnp.float32(0.0))
-        pairs = [(p * col_count + q, (p ^ 1) * col_count + q) for p in range(row_count) for q in range(col_count)]
+        senders = range(0, row_count, 2) if len(group) == 1 else range(row_count)
+        pairs = [(p * col_count + q, (p ^ 1) * col_count + q) for p in senders for q in range(col_count)]
         other = lax.ppermute(held, ("row", "col"), pairs)
         for a in group:
             band = jnp.where(odd == (a % 2 == 1), held, other)

time: 294 us -> 295 us (level)
  transfers between devices with their start and end apart: 19 -> 19, of which waited for: 2 -> 2; matrix products, arithmetic and copies ran while one was open for 65% -> 64% of each run, Pallas kernels for 0% -> 0%
where the time goes in v2:
time: 295 us; the launch traced here: 289 us
  other arithmetic  155 us (53%)
  matrix products  62 us (21%)
  waiting for transfers between devices  25.7 us (9%)
  starting transfers between devices  17.9 us (6%)
  between operations  15.6 us (5%)
  local copies, waits for them, and re-layouts  12.7 us (4%)
    another operation x9, other arithmetic, factor_block(): bottom = jnp.linalg.cholesky(schur[half:, half:] - mul(side, side, True))  37.6 us
    another operation x9, other arithmetic, factor_block(): top = jnp.linalg.cholesky(schur[:half, :half])  37.2 us
    another operation x6, other arithmetic, factor_block(): top_inv = jax.scipy.linalg.solve_triangular(top, eye, lower=True)  32 us
    another operation x6, other arithmetic, factor_block(): bottom_inv = jax.scipy.linalg.solve_triangular(bottom, eye, lower=True)  31.4 us
    dot_general x6, matrix products, apply_inverse(): lax.dot_general(piece, inverse[j * BLOCK:hi, :hi], (((axis,), (1,)), ((),...  26.5 us
    dot_general x1, matrix products, shards(): lax.dot_general(panels, across, (((1,), (1,)), ((), ())), precision=lax.P...  23.2 us
    ppermute x6, waiting for transfers between devices, gather_corner(): got = lax.ppermute(mine, ('row', 'col'), pairs)  22.2 us
    dot_general x26, matrix products, mul(): lax.dot_general(a, b, dims, precision=lax.Precision.HIGHEST, preferred_el...  10.7 us
  transfers between devices with their start and end apart: 19, of which 2 were waited for; matrix products, arithmetic and copies ran while one was open for 64% of the time, Pallas kernels for 0%

profile of v2, /device:TPU:10, one launch (start us, length us, event | category | flops | bytes accessed | tf_op | source)
XLA Modules:
  0.0 288.9 jit_solution(10492667905597582636)
XLA Ops:
  7.6 1.3 select_dynamic-update-slice_fusion.1
  8.9 1.7 copy-done.3
  10.7 1.0 slice.75
  11.6 0.7 collective-permute-start.2
  12.3 0.7 collective-permute-start.1
  13.0 0.7 collective-permute-start
  13.8 1.1 select_add_fusion.2
  15.0 0.7 collective-permute-start.5
  15.7 0.7 collective-permute-start.4
  16.3 0.7 collective-permute-start.3
  17.0 3.1 %broadcast_in_dim.81 = f32[2048,768]{1,0:T(8,128)} broadcast(f32[]{:T(128)} %constant.252.clone.1), dimensions={} | broadcast | bytes 6291460 | tf_op jit(solution)/shard_map/broadcast_in_dim | solution.py:73
  20.1 3.2 %select_dynamic-update-slice_fusion = f32[2048,768]{1,0:T(8,128)} fusion(f32[2048,768]{1,0:T(8,128)} %broadcast_in_dim.81, s32[]{:T(128)S(6)} %select_n.491, f32[2048,1024]{1,0:T(8,128)} %param.4, pred[]{:T(512)S(6)} %lt.164), kind=kLoop, calls=%fused_computation.33 | loop fusion | flops 524288 | bytes 4194309 | tf_op jit(solution)/shard_map/dynamic_update_slice | solution.py:74
  23.6 0.7 collective-permute-start.12
  24.3 1.5 collective-permute-start.11
  25.8 1.3 collective-permute-start.10
  27.2 0.7 collective-permute-start.8
  28.2 0.7 collective-permute-start.7
  28.9 1.3 collective-permute-start.6
  30.2 1.4 iota_compare_fusion
  31.5 22.2 %collective-permute-done.6 = f32[256,256]{1,0:T(8,128)S(1)} collective-permute-done((f32[256,256]{1,0:T(8,128)S(1)}, f32[256,256]{1,0:T(8,128)S(1)}, u32[]{:S(2)}, u32[]{:S(2)}) %collective-permute-start.6) | collective-permute-done | bytes 262176 | tf_op jit(solution)/shard_map/ppermute | solution.py:57
  53.8 1.3 collective-permute-start.9
  55.1 3.4 %collective-permute-done.10 = f32[256,768]{1,0:T(8,128)} collective-permute-done((f32[256,768]{1,0:T(8,128)S(1)}, f32[256,768]{1,0:T(8,128)}, u32[]{:S(2)}, u32[]{:S(2)}) %collective-permute-start.10) | collective-permute-done | bytes 786464 | tf_op jit(solution)/shard_map/ppermute | solution.py:47
  58.5 1.4 select_add_fusion.1
  59.9 1.3 collective-permute-start.15
  61.3 2.2 collective-permute-start.14
  63.4 2.6 collective-permute-start.13
  66.3 11.7 %cholesky.104 = f32[128,128]{1,0:T(8,128)S(1)} custom-call(f32[128,128]{1,0:T(8,128)S(1)} %copy.4), custom_call_target="Cholesky" | custom-call | tf_op jit(solution)/shard_map/jit(cholesky)/cholesky | solution.py:95
  79.3 9.8 %custom-call.10 = f32[1,128,128]{1,2,0:T(8,128)S(1)} custom-call(f32[1,128,128]{2,1,0:T(8,128)S(1)} %get-tuple-element.14), custom_call_target="InvertDiagBlocksLowerTriangular" | custom-call | tf_op jit(solution)/shard_map/jit(_solve_triangular)/triangular_solve | solution.py:96
  90.3 11.7 %cholesky.115 = f32[128,128]{1,0:T(8,128)S(1)} custom-call(f32[128,128]{1,0:T(8,128)S(1)} %copy.6), custom_call_target="Cholesky" | custom-call | tf_op jit(solution)/shard_map/jit(cholesky)/cholesky | solution.py:98
  103.3 9.9 %custom-call.11 = f32[1,128,128]{1,2,0:T(8,128)S(1)} custom-call(f32[1,128,128]{2,1,0:T(8,128)S(1)} %get-tuple-element.12), custom_call_target="InvertDiagBlocksLowerTriangular" | custom-call | tf_op jit(solution)/shard_map/jit(_solve_triangular)/triangular_solve | solution.py:99
  113.5 0.9 copy-done.10
  114.7 0.7 select_maximum_fusion.1
  116.1 4.0 %fusion.14 = f32[1024,256]{1,0:T(8,128)} fusion(f32[768,1024]{1,0:T(8,128)} %all-reduce.14.cloned.1.call-done, f32[128,128]{1,0:T(8,128)S(1)} %fusion.53, f32[128,128]{1,0:T(8,128)S(1)} %copy.9, f32[128,128]{1,0:T(8,128)S(1)} %convolution_negate_fusion.5), kind=kOutput, calls=%fused_computation.41 | convolution fusion | flops 805568512 | bytes 2293760 | tf_op jit(solution)/shard_map/dot_general | solution.py:148
  120.1 1.2 broadcast_select_fusion.1
  122.6 11.7 %cholesky.126 = f32[128,128]{1,0:T(8,128)S(1)} custom-call(f32[128,128]{1,0:T(8,128)S(1)} %copy.11), custom_call_target="Cholesky" | custom-call | tf_op jit(solution)/shard_map/jit(cholesky)/cholesky | solution.py:95
  134.4 0.7 compare_reduce_fusion.3
  135.1 1.3 select_bitcast_fusion.3
  136.3 9.8 %custom-call.12 = f32[1,128,128]{1,2,0:T(8,128)S(1)} custom-call(f32[1,128,128]{2,1,0:T(8,128)S(1)} %get-tuple-element.10), custom_call_target="InvertDiagBlocksLowerTriangular" | custom-call | tf_op jit(solution)/shard_map/jit(_solve_triangular)/triangular_solve | solution.py:96
  148.5 12.1 %cholesky.137 = f32[128,128]{1,0:T(8,128)S(1)} custom-call(f32[128,128]{1,0:T(8,128)S(1)} %copy.13), custom_call_target="Cholesky" | custom-call | tf_op jit(solution)/shard_map/jit(cholesky)/cholesky | solution.py:98
  160.6 0.7 compare_reduce_fusion.2
  161.3 0.6 select_bitcast_fusion.2
  162.0 9.8 %custom-call.13 = f32[1,128,128]{1,2,0:T(8,128)S(1)} custom-call(f32[1,128,128]{2,1,0:T(8,128)S(1)} %get-tuple-element.8), custom_call_target="InvertDiagBlocksLowerTriangular" | custom-call | tf_op jit(solution)/shard_map/jit(_solve_triangular)/triangular_solve | solution.py:99
  172.5 0.8 copy.15
  173.4 0.8 copy.23
  174.6 0.8 copy.24
  176.9 11.7 %cholesky.148 = f32[128,128]{1,0:T(8,128)S(1)} custom-call(f32[128,128]{1,0:T(8,128)S(1)} %copy.19), custom_call_target="Cholesky" | custom-call | tf_op jit(solution)/shard_map/jit(cholesky)/cholesky | solution.py:95
  188.7 0.7 compare_reduce_fusion.1
  189.3 0.7 select_bitcast_fusion.1
  190.0 9.9 %custom-call.14 = f32[1,128,128]{1,2,0:T(8,128)S(1)} custom-call(f32[1,128,128]{2,1,0:T(8,128)S(1)} %get-tuple-element.6), custom_call_target="InvertDiagBlocksLowerTriangular" | custom-call | tf_op jit(solution)/shard_map/jit(_solve_triangular)/triangular_solve | solution.py:96
  200.5 0.7 copy.22
  201.8 11.7 %cholesky.159 = f32[128,128]{1,0:T(8,128)S(1)} custom-call(f32[128,128]{1,0:T(8,128)S(1)} %copy.21), custom_call_target="Cholesky" | custom-call | tf_op jit(solution)/shard_map/jit(cholesky)/cholesky | solution.py:98
  213.5 0.7 compare_reduce_fusion
  214.2 0.6 select_bitcast_fusion
  214.8 9.8 %custom-call.15 = f32[1,128,128]{1,2,0:T(8,128)S(1)} custom-call(f32[1,128,128]{2,1,0:T(8,128)S(1)} %get-tuple-element.4), custom_call_target="InvertDiagBlocksLowerTriangular" | custom-call | tf_op jit(solution)/shard_map/jit(_solve_triangular)/triangular_solve | solution.py:99
  225.0 1.0 pad_select_fusion
  226.1 3.1 %fusion.24 = f32[256,768]{1,0:T(8,128)} fusion(s32[]{:T(128)S(6)} %select_n.488, f32[256,256]{1,0:T(8,128)S(1)} %copy-done.8, f32[128,128]{1,0:T(8,128)S(1)} %copy.14, f32[128,128]{1,0:T(8,128)S(1)} %get-tuple-element.9, f32[256,256]{1,0:T(8,128)S(1)} %broadcast_in_dim.79, f32[256,256]{1,0:T(8,128)S(1)} %copy-done.9, f32[256,256]{1,0:T(8,128)} %copy.24, ...), kind=kLoop, calls=%fused_computation.55 | loop fusion | flops 3735552 | bytes 3802112 | tf_op jit(solution)/shard_map/concatenate | solution.py:134
  233.6 3.5 %fusion.10 = f32[1024,256]{1,0:T(8,128)S(1)} fusion(f32[768,1024]{1,0:T(8,128)S(1)} %copy-done.2, f32[128,128]{1,0:T(8,128)S(1)} %copy.17, f32[128,128]{1,0:T(8,128)S(1)} %convolution_negate_fusion.4, f32[128,256]{1,0:T(8,128)S(1)} %concatenate.99, f32[256,256]{1,0:T(8,128)S(1)} %convolution_negate_fusion.2), kind=kOutput, calls=%fused_computation.29 | convolution fusion | flops 1611005952 | bytes 3670016 | tf_op jit(solution)/shard_map/dot_general | solution.py:148
  237.1 5.2 %fusion.35 = f32[1024,256]{1,0:T(8,128)S(1)} fusion(f32[768,1024]{1,0:T(8,128)S(1)} %copy-done.2, f32[128,128]{1,0:T(8,128)S(1)} %copy.27, f32[128,128]{1,0:T(8,128)S(1)} %convolution_negate_fusion.3, f32[128,256]{1,0:T(8,128)S(1)} %concatenate.108, f32[256,256]{1,0:T(8,128)S(1)} %convolution_negate_fusion, f32[256,256]{1,0:T(8,128)S(1)} %convolution_negate_fusion.1), kind=kOutput, calls=%fused_computation.77 | convolution fusion | flops 2416705536 | bytes 4980736 | tf_op jit(solution)/shard_map/dot_general | solution.py:148
  242.4 8.1 %fusion.36 = f32[2048,256]{1,0:T(8,128)S(1)} fusion(f32[2048,768]{1,0:T(8,128)} %all-reduce.12.cloned.1.call-done, f32[128,128]{1,0:T(8,128)S(1)} %copy.27, f32[128,128]{1,0:T(8,128)} %copy-done.6, f32[128,256]{1,0:T(8,128)S(1)} %concatenate.108, f32[256,256]{1,0:T(8,128)S(1)} %convolution_negate_fusion, f32[256,256]{1,0:T(8,128)S(1)} %convolution_negate_fusion.1), kind=kOutput, calls=%fused_computation.78 | convolution fusion | flops 4832624640 | bytes 9175040 | tf_op jit(solution)/shard_map/dot_general | solution.py:148
  250.5 3.7 %fusion = f32[2048,256]{1,0:T(8,128)S(1)} fusion(f32[2048,768]{1,0:T(8,128)S(1)} %copy-done, f32[128,128]{1,0:T(8,128)S(1)} %copy.17, f32[128,128]{1,0:T(8,128)S(1)} %convolution_negate_fusion.4, f32[128,256]{1,0:T(8,128)S(1)} %concatenate.99, f32[256,256]{1,0:T(8,128)S(1)} %convolution_negate_fusion.2), kind=kOutput, calls=%fused_computation.2 | convolution fusion | flops 3221618688 | bytes 6815744 | tf_op jit(solution)/shard_map/dot_general | solution.py:148
  254.2 1.9 fusion.12
  256.2 1.5 maximum_select_fusion
  257.8 0.7 slice-done.1
  258.7 23.2 %subtract_select_fusion = f32[2048,1024]{1,0:T(8,128)} fusion(f32[2048,1024]{1,0:T(8,128)S(1)} %bitcast.95, pred[1024]{0:T(1024)(128)(4,1)S(1)} %fusion.83, pred[2048]{0:T(1024)(128)(4,1)S(1)} %fusion.76, f32[2048,768]{1,0:T(8,128)S(1)} %maximum_select_fusion, f32[1024,256]{1,0:T(8,128)S(1)} %fusion.35, f32[1024,256]{1,0:T(8,128)S(1)} %fusion.10, ...), kind=kOutput, calls=%fused_computation | convolution fusion | flops 19335217152 | bytes 26217472 | tf_op jit(solution)/shard_map/dot_general | solution.py:176
  (127 shorter events, 18.2 us)
Async XLA Ops:
  7.2 109.0 %all-reduce.14.cloned.1.call-start = ((), (), s32[]{:S(2)}) async-start(), calls=%async_computation.1 | async-start | bytes 6291456 | tf_op jit(solution)/shard_map/psum | solution.py:84
  8.9 1.7 copy-start.3
  10.6 231.7 %all-reduce.12.cloned.1.call-start = ((), (), s32[]{:S(2)}) async-start(), calls=%async_computation | async-start | bytes 12582912 | tf_op jit(solution)/shard_map/psum | solution.py:75
  11.6 2.2 collective-permute-start.2
  12.3 1.5 collective-permute-start.1
  13.0 0.8 collective-permute-start
  15.0 10.9 %collective-permute-start.5 = (f32[256,256]{1,0:T(8,128)S(1)}, f32[256,256]{1,0:T(8,128)S(1)}, u32[]{:S(2)}, u32[]{:S(2)}) collective-permute-start(f32[256,256]{1,0:T(8,128)S(1)} %get-tuple-element.20), channel_id=1, source_target_pairs={{0,12},{1,13},{2,14},{3,15}} | collective-permute-start | bytes 786440 | tf_op jit(solution)/shard_map/ppermute | solution.py:47
  15.7 11.5 %collective-permute-start.4 = (f32[256,256]{1,0:T(8,128)S(1)}, f32[256,256]{1,0:T(8,128)S(1)}, u32[]{:S(2)}, u32[]{:S(2)}) collective-permute-start(f32[256,256]{1,0:T(8,128)S(1)} %get-tuple-element.20), channel_id=1, source_target_pairs={{0,8},{1,9},{2,10},{3,11}} | collective-permute-start | bytes 786440 | tf_op jit(solution)/shard_map/ppermute | solution.py:47
  16.3 10.8 %collective-permute-start.3 = (f32[256,256]{1,0:T(8,128)S(1)}, f32[256,256]{1,0:T(8,128)S(1)}, u32[]{:S(2)}, u32[]{:S(2)}) collective-permute-start(f32[256,256]{1,0:T(8,128)S(1)} %get-tuple-element.20), channel_id=1, source_target_pairs={{0,4},{1,5},{2,6},{3,7}} | collective-permute-start | bytes 786440 | tf_op jit(solution)/shard_map/ppermute | solution.py:47
  23.6 31.5 %collective-permute-start.12 = (f32[256,768]{1,0:T(8,128)S(1)}, f32[256,768]{1,0:T(8,128)S(1)}, u32[]{:S(2)}, u32[]{:S(2)}) collective-permute-start(f32[256,768]{1,0:T(8,128)S(1)} %fusion.18), channel_id=1, source_target_pairs={{16,28},{17,29},{18,30},{19,31},{32,44},{33,45},{34,46},{35,47}} | collective-permute-start | bytes 2359304 | tf_op jit(solution)/shard_map/ppermute | solution.py:47
  24.3 30.8 %collective-permute-start.11 = (f32[256,768]{1,0:T(8,128)S(1)}, f32[256,768]{1,0:T(8,128)}, u32[]{:S(2)}, u32[]{:S(2)}) collective-permute-start(f32[256,768]{1,0:T(8,128)S(1)} %fusion.18), channel_id=1, source_target_pairs={{16,24},{17,25},{18,26},{19,27},{32,40},{33,41},{34,42},{35,43}} | collective-permute-start | bytes 2359304 | tf_op jit(solution)/shard_map/ppermute | solution.py:47
  25.8 32.7 %collective-permute-start.10 = (f32[256,768]{1,0:T(8,128)S(1)}, f32[256,768]{1,0:T(8,128)}, u32[]{:S(2)}, u32[]{:S(2)}) collective-permute-start(f32[256,768]{1,0:T(8,128)S(1)} %fusion.18), channel_id=1, source_target_pairs={{16,20},{17,21},{18,22},{19,23},{32,36},{33,37},{34,38},{35,39}} | collective-permute-start | bytes 2359304 | tf_op jit(solution)/shard_map/ppermute | solution.py:47
  27.2 1.6 collective-permute-start.8
  28.2 3.4 %collective-permute-start.7 = (f32[256,256]{1,0:T(8,128)S(1)}, f32[256,256]{1,0:T(8,128)S(1)}, u32[]{:S(2)}, u32[]{:S(2)}) collective-permute-start(f32[256,256]{1,0:T(8,128)S(1)} %select_add_fusion.5), channel_id=1, source_target_pairs={{0,64},{1,65},{2,66},{3,67},{4,68},{5,69},{6,70},{7,71},{8,72},{9,... | collective-permute-start | bytes 786440 | tf_op jit(solution)/shard_map/ppermute | solution.py:57
  28.9 24.8 %collective-permute-start.6 = (f32[256,256]{1,0:T(8,128)S(1)}, f32[256,256]{1,0:T(8,128)S(1)}, u32[]{:S(2)}, u32[]{:S(2)}) collective-permute-start(f32[256,256]{1,0:T(8,128)S(1)} %select_add_fusion.5), channel_id=1, source_target_pairs={{0,32},{1,33},{2,34},{3,35},{4,36},{5,37},{6,38},{7,39},{8,40},{9,... | collective-permute-start | bytes 786440 | tf_op jit(solution)/shard_map/ppermute | solution.py:57
  53.8 12.3 %collective-permute-start.9 = (f32[256,256]{1,0:T(8,128)S(1)}, f32[256,256]{1,0:T(8,128)S(1)}, u32[]{:S(2)}, u32[]{:S(2)}) collective-permute-start(f32[256,256]{1,0:T(8,128)S(1)} %select_add_fusion.4), channel_id=1, source_target_pairs={{0,16},{1,17},{2,18},{3,19},{4,20},{5,21},{6,22},{7,23},{8,24},{9,... | collective-permute-start | bytes 786440 | tf_op jit(solution)/shard_map/ppermute | solution.py:62
  59.9 53.6 %collective-permute-start.15 = (f32[256,768]{1,0:T(8,128)S(1)}, f32[256,768]{1,0:T(8,128)S(1)}, u32[]{:S(2)}, u32[]{:S(2)}) collective-permute-start(f32[256,768]{1,0:T(8,128)S(1)} %select_add_fusion.1), channel_id=1, source_target_pairs={{16,112},{17,113},{18,114},{19,115},{20,116},{21,117},{22,118},{23... | collective-permute-start | bytes 2359304 | tf_op jit(solution)/shard_map/ppermute | solution.py:57
  61.3 52.3 %collective-permute-start.14 = (f32[256,768]{1,0:T(8,128)S(1)}, f32[256,768]{1,0:T(8,128)}, u32[]{:S(2)}, u32[]{:S(2)}) collective-permute-start(f32[256,768]{1,0:T(8,128)S(1)} %select_add_fusion.1), channel_id=1, source_target_pairs={{16,80},{17,81},{18,82},{19,83},{20,84},{21,85},{22,86},{23,87},{2... | collective-permute-start | bytes 2359304 | tf_op jit(solution)/shard_map/ppermute | solution.py:57
  63.4 51.0 %collective-permute-start.13 = (f32[256,768]{1,0:T(8,128)S(1)}, f32[256,768]{1,0:T(8,128)}, u32[]{:S(2)}, u32[]{:S(2)}) collective-permute-start(f32[256,768]{1,0:T(8,128)S(1)} %select_add_fusion.1), channel_id=1, source_target_pairs={{16,48},{17,49},{18,50},{19,51},{20,52},{21,53},{22,54},{23,55},{2... | collective-permute-start | bytes 2359304 | tf_op jit(solution)/shard_map/ppermute | solution.py:57
  113.5 0.9 copy-start.10
  114.6 5.5 %collective-permute-start.16 = (f32[256,768]{1,0:T(8,128)S(1)}, f32[256,768]{1,0:T(8,128)}, u32[]{:S(2)}, u32[]{:S(2)}) collective-permute-start(f32[256,768]{1,0:T(8,128)S(1)} %select_add_fusion), channel_id=1, source_target_pairs={{0,16},{1,17},{2,18},{3,19},{4,20},{5,21},{6,22},{7,23},{8,24},{9,... | collective-permute-start | bytes 2359304 | tf_op jit(solution)/shard_map/ppermute | solution.py:62
  176.1 50.0 %copy-start.7 = (f32[256,256]{1,0:T(8,128)S(1)}, f32[256,256]{1,0:T(8,128)}, u32[]{:S(2)}) copy-start(f32[256,256]{1,0:T(8,128)} %select_maximum_fusion.1) | copy-start | bytes 786436
  176.7 49.4 %copy-start.8 = (f32[256,256]{1,0:T(8,128)S(1)}, f32[256,256]{1,0:T(8,128)}, u32[]{:S(2)}) copy-start(f32[256,256]{1,0:T(8,128)} %copy.15) | copy-start | bytes 786436
  176.7 49.4 %copy-start.9 = (f32[256,256]{1,0:T(8,128)S(1)}, f32[256,256]{1,0:T(8,128)}, u32[]{:S(2)}) copy-start(f32[256,256]{1,0:T(8,128)} %copy.23) | copy-start | bytes 786436
  229.2 4.4 %copy-start.2 = (f32[768,1024]{1,0:T(8,128)S(1)}, f32[768,1024]{1,0:T(8,128)}, u32[]{:S(2)}) copy-start(f32[768,1024]{1,0:T(8,128)} %all-reduce.14.cloned.1.call-done) | copy-start | bytes 9437188
  229.8 7.3 %copy-start.6 = (f32[128,128]{1,0:T(8,128)}, f32[128,128]{1,0:T(8,128)S(1)}, u32[]{:S(2)}) copy-start(f32[128,128]{1,0:T(8,128)S(1)} %convolution_negate_fusion.3) | copy-start | bytes 196612
  242.4 8.1 %copy-start = (f32[2048,768]{1,0:T(8,128)S(1)}, f32[2048,768]{1,0:T(8,128)}, u32[]{:S(2)}) copy-start(f32[2048,768]{1,0:T(8,128)} %all-reduce.12.cloned.1.call-done) | copy-start | bytes 18874372
  250.5 5.7 %copy-start.5 = (f32[256,768]{1,0:T(8,128)S(1)}, f32[256,768]{1,0:T(8,128)}, u32[]{:S(2)}) copy-start(f32[256,768]{1,0:T(8,128)} %fusion.24) | copy-start | bytes 2359300
  254.2 3.5 %slice-start = ((s8[8388608]{0:T(1024)(128)(4,1)}), s8[4194304]{0:T(1024)(128)(4,1)S(1)}, s32[]{:S(2)}) async-start(s8[8388608]{0:T(1024)(128)(4,1)} %bitcast.94), calls=%async_computation.2 | async-start | bytes 8388608
  256.2 2.3 slice-start.1
  256.2 2.5 copy-start.4
  258.7 23.2 %copy-start.1 = (f32[2048,768]{1,0:T(8,128)}, f32[2048,768]{1,0:T(8,128)S(1)}, u32[]{:S(2)}) copy-start(f32[2048,768]{1,0:T(8,128)S(1)} %maximum_select_fusion) | copy-start | bytes 18874372
Sparse Core Ops, SparseCore 0:
  10.9 78.7 all-reduce.13
  93.8 125.2 all-reduce.11

commit v3 on v1

--- a/solution.py
+++ b/solution.py
@@ -167,13 +167,20 @@
 
     factor, inverse = factor_corner(blocks)
     panels = apply_inverse(band_cols, inverse, 1)
-    across = apply_inverse(band_rows, inverse, 0)
+    across = jnp.concatenate([
+        lax.dot_general(
+            inverse[j * BLOCK:(j + 1) * BLOCK, :(j + 1) * BLOCK], band_rows[:(j + 1) * BLOCK],
+            (((1,), (0,)), ((), ())),
+            precision=lax.Precision.HIGHEST, preferred_element_type=jnp.float32,
+        )
+        for j in range(STEPS)
+    ], axis=0)
     own = lax.dynamic_slice_in_dim(factor, jnp.minimum(row_index, STEPS - 1) * BLOCK, BLOCK, 0)
     own = jnp.pad(own, ((0, rows_local - BLOCK), (0, 0)))
     head = (jnp.arange(rows_local) < BLOCK)[:, None] & (row_index < STEPS)
     panels = jnp.where(head, own, panels)
     update = lax.dot_general(
-        panels, across, (((1,), (1,)), ((), ())),
+        panels, across, (((1,), (0,)), ((), ())),
         precision=lax.Precision.HIGHEST, preferred_element_type=jnp.float32,
     )
     keep = (row_ids >= STEPS)[:, None] & (col_ids >= STEPS)[None, :]

time: 294 us -> 289 us (0.983)
  matrix products: 62 us -> 56.8 us
    dot_general x6 -> x3, matrix products: 26.3 us -> 13.4 us  [apply_inverse(): lax.dot_general(piece, inverse[j * BLOCK:hi, :hi], (((axis,), (1,)), ((),...]
    dot_general x1 -> x4, matrix products: 23.2 us -> 31.1 us  [the longest x1 23.2 us: shards(): lax.dot_general(panels, across, (((1,), (0,)), ((), ())), precision=lax.P...]
  transfers between devices with their start and end apart: 19 -> 19, of which waited for: 2 -> 2; matrix products, arithmetic and copies ran while one was open for 65% -> 64% of each run, Pallas kernels for 0% -> 0%
where the time goes in v3:
time: 289 us; the launch traced here: 284 us
  other arithmetic  155 us (54%)
  matrix products  56.8 us (20%)
  waiting for transfers between devices  26.9 us (9%)
  starting transfers between devices  16.3 us (6%)
  between operations  15.6 us (5%)
  local copies, waits for them, and re-layouts  12.7 us (4%)
    another operation x9, other arithmetic, factor_block(): bottom = jnp.linalg.cholesky(schur[half:, half:] - mul(side, side, True))  37.4 us
    another operation x9, other arithmetic, factor_block(): top = jnp.linalg.cholesky(schur[:half, :half])  37.2 us
    another operation x6, other arithmetic, factor_block(): top_inv = jax.scipy.linalg.solve_triangular(top, eye, lower=True)  32.3 us
    another operation x6, other arithmetic, factor_block(): bottom_inv = jax.scipy.linalg.solve_triangular(bottom, eye, lower=True)  31.7 us
    dot_general x1, matrix products, shards(): lax.dot_general(panels, across, (((1,), (0,)), ((), ())), precision=lax.P...  23.2 us
    ppermute x6, waiting for transfers between devices, gather_corner(): got = lax.ppermute(mine, ('row', 'col'), pairs)  22.2 us
    dot_general x3, matrix products, apply_inverse(): lax.dot_general(piece, inverse[j * BLOCK:hi, :hi], (((axis,), (1,)), ((),...  13.4 us
    dot_general x26, matrix products, mul(): lax.dot_general(a, b, dims, precision=lax.Precision.HIGHEST, preferred_el...  10.7 us
  transfers between devices with their start and end apart: 19, of which 2 were waited for; matrix products, arithmetic and copies ran while one was open for 64% of the time, Pallas kernels for 0%

profile of v3, /device:TPU:10, one launch (start us, length us, event | category | flops | bytes accessed | tf_op | source)
XLA Modules:
  0.0 283.7 jit_solution(5477114605221803457)
XLA Ops:
  7.6 1.3 select_dynamic-update-slice_fusion.1
  8.9 1.7 copy-done.3
  10.7 1.0 slice.75
  11.6 0.7 collective-permute-start.2
  12.3 0.7 collective-permute-start.1
  13.0 0.7 collective-permute-start
  13.8 1.1 select_add_fusion.2
  15.0 0.7 collective-permute-start.5
  15.7 0.7 collective-permute-start.4
  16.3 0.7 collective-permute-start.3
  17.0 3.1 %broadcast_in_dim.81 = f32[2048,768]{1,0:T(8,128)} broadcast(f32[]{:T(128)} %constant.252.clone.1), dimensions={} | broadcast | bytes 6291460 | tf_op jit(solution)/shard_map/broadcast_in_dim | solution.py:72
  20.1 3.2 %select_dynamic-update-slice_fusion = f32[2048,768]{1,0:T(8,128)} fusion(f32[2048,768]{1,0:T(8,128)} %broadcast_in_dim.81, s32[]{:T(128)S(6)} %select_n.491, f32[2048,1024]{1,0:T(8,128)} %param.4, pred[]{:T(512)S(6)} %lt.164), kind=kLoop, calls=%fused_computation.33 | loop fusion | flops 524288 | bytes 4194309 | tf_op jit(solution)/shard_map/dynamic_update_slice | solution.py:73
  23.6 0.7 collective-permute-start.12
  24.3 1.5 collective-permute-start.11
  25.8 1.3 collective-permute-start.10
  27.2 0.7 collective-permute-start.8
  28.2 0.7 collective-permute-start.7
  28.9 1.3 collective-permute-start.6
  30.2 1.4 iota_compare_fusion
  31.5 22.2 %collective-permute-done.6 = f32[256,256]{1,0:T(8,128)S(1)} collective-permute-done((f32[256,256]{1,0:T(8,128)S(1)}, f32[256,256]{1,0:T(8,128)S(1)}, u32[]{:S(2)}, u32[]{:S(2)}) %collective-permute-start.6) | collective-permute-done | bytes 262176 | tf_op jit(solution)/shard_map/ppermute | solution.py:57
  53.9 4.7 %collective-permute-done.10 = f32[256,768]{1,0:T(8,128)} collective-permute-done((f32[256,768]{1,0:T(8,128)S(1)}, f32[256,768]{1,0:T(8,128)}, u32[]{:S(2)}, u32[]{:S(2)}) %collective-permute-start.10) | collective-permute-done | bytes 786464 | tf_op jit(solution)/shard_map/ppermute | solution.py:47
  58.5 1.4 select_add_fusion.1
  59.9 1.3 collective-permute-start.15
  61.3 2.2 collective-permute-start.14
  63.4 2.3 collective-permute-start.13
  66.1 11.7 %cholesky.104 = f32[128,128]{1,0:T(8,128)S(1)} custom-call(f32[128,128]{1,0:T(8,128)S(1)} %copy.4), custom_call_target="Cholesky" | custom-call | tf_op jit(solution)/shard_map/jit(cholesky)/cholesky | solution.py:94
  79.0 9.8 %custom-call.10 = f32[1,128,128]{1,2,0:T(8,128)S(1)} custom-call(f32[1,128,128]{2,1,0:T(8,128)S(1)} %get-tuple-element.14), custom_call_target="InvertDiagBlocksLowerTriangular" | custom-call | tf_op jit(solution)/shard_map/jit(_solve_triangular)/triangular_solve | solution.py:95
  90.0 11.7 %cholesky.115 = f32[128,128]{1,0:T(8,128)S(1)} custom-call(f32[128,128]{1,0:T(8,128)S(1)} %copy.6), custom_call_target="Cholesky" | custom-call | tf_op jit(solution)/shard_map/jit(cholesky)/cholesky | solution.py:97
  103.0 10.2 %custom-call.11 = f32[1,128,128]{1,2,0:T(8,128)S(1)} custom-call(f32[1,128,128]{2,1,0:T(8,128)S(1)} %get-tuple-element.12), custom_call_target="InvertDiagBlocksLowerTriangular" | custom-call | tf_op jit(solution)/shard_map/jit(_solve_triangular)/triangular_solve | solution.py:98
  113.5 0.9 copy-done.10
  114.6 0.7 select_maximum_fusion.1
  116.1 3.2 %fusion.14 = f32[256,1024]{1,0:T(8,128)} fusion(f32[768,1024]{1,0:T(8,128)} %all-reduce.14.cloned.1.call-done, f32[128,128]{1,0:T(8,128)S(1)} %fusion.53, f32[128,128]{1,0:T(8,128)S(1)} %copy.9, f32[128,128]{1,0:T(8,128)S(1)} %convolution_negate_fusion.5), kind=kOutput, calls=%fused_computation.41 | convolution fusion | flops 805568512 | bytes 2293760 | tf_op jit(solution)/shard_map/dot_general | solution.py:171
  119.3 1.3 broadcast_select_fusion.1
  121.8 11.7 %cholesky.126 = f32[128,128]{1,0:T(8,128)S(1)} custom-call(f32[128,128]{1,0:T(8,128)S(1)} %copy.11), custom_call_target="Cholesky" | custom-call | tf_op jit(solution)/shard_map/jit(cholesky)/cholesky | solution.py:94
  133.6 0.7 compare_reduce_fusion.3
  134.2 1.3 select_bitcast_fusion.3
  135.5 9.8 %custom-call.12 = f32[1,128,128]{1,2,0:T(8,128)S(1)} custom-call(f32[1,128,128]{2,1,0:T(8,128)S(1)} %get-tuple-element.10), custom_call_target="InvertDiagBlocksLowerTriangular" | custom-call | tf_op jit(solution)/shard_map/jit(_solve_triangular)/triangular_solve | solution.py:95
  147.7 11.9 %cholesky.137 = f32[128,128]{1,0:T(8,128)S(1)} custom-call(f32[128,128]{1,0:T(8,128)S(1)} %copy.13), custom_call_target="Cholesky" | custom-call | tf_op jit(solution)/shard_map/jit(cholesky)/cholesky | solution.py:97
  159.6 0.7 compare_reduce_fusion.2
  160.3 0.6 select_bitcast_fusion.2
  160.9 9.8 %custom-call.13 = f32[1,128,128]{1,2,0:T(8,128)S(1)} custom-call(f32[1,128,128]{2,1,0:T(8,128)S(1)} %get-tuple-element.8), custom_call_target="InvertDiagBlocksLowerTriangular" | custom-call | tf_op jit(solution)/shard_map/jit(_solve_triangular)/triangular_solve | solution.py:98
  171.4 0.8 copy.15
  172.4 0.8 copy.23
  173.6 0.8 copy.24
  175.9 11.7 %cholesky.148 = f32[128,128]{1,0:T(8,128)S(1)} custom-call(f32[128,128]{1,0:T(8,128)S(1)} %copy.19), custom_call_target="Cholesky" | custom-call | tf_op jit(solution)/shard_map/jit(cholesky)/cholesky | solution.py:94
  187.7 0.7 compare_reduce_fusion.1
  188.3 0.6 select_bitcast_fusion.1
  189.0 10.2 %custom-call.14 = f32[1,128,128]{1,2,0:T(8,128)S(1)} custom-call(f32[1,128,128]{2,1,0:T(8,128)S(1)} %get-tuple-element.6), custom_call_target="InvertDiagBlocksLowerTriangular" | custom-call | tf_op jit(solution)/shard_map/jit(_solve_triangular)/triangular_solve | solution.py:95
  199.7 0.7 copy.22
  201.0 11.7 %cholesky.159 = f32[128,128]{1,0:T(8,128)S(1)} custom-call(f32[128,128]{1,0:T(8,128)S(1)} %copy.21), custom_call_target="Cholesky" | custom-call | tf_op jit(solution)/shard_map/jit(cholesky)/cholesky | solution.py:97
  212.7 0.7 compare_reduce_fusion
  213.4 0.6 select_bitcast_fusion
  214.0 9.8 %custom-call.15 = f32[1,128,128]{1,2,0:T(8,128)S(1)} custom-call(f32[1,128,128]{2,1,0:T(8,128)S(1)} %get-tuple-element.4), custom_call_target="InvertDiagBlocksLowerTriangular" | custom-call | tf_op jit(solution)/shard_map/jit(_solve_triangular)/triangular_solve | solution.py:98
  224.2 1.0 pad_select_fusion
  225.3 3.1 %fusion.24 = f32[256,768]{1,0:T(8,128)} fusion(s32[]{:T(128)S(6)} %select_n.488, f32[256,256]{1,0:T(8,128)S(1)} %copy-done.8, f32[128,128]{1,0:T(8,128)S(1)} %copy.14, f32[128,128]{1,0:T(8,128)S(1)} %get-tuple-element.9, f32[256,256]{1,0:T(8,128)S(1)} %broadcast_in_dim.79, f32[256,256]{1,0:T(8,128)S(1)} %copy-done.9, f32[256,256]{1,0:T(8,128)} %copy.24, ...), kind=kLoop, calls=%fused_computation.55 | loop fusion | flops 3735552 | bytes 3802112 | tf_op jit(solution)/shard_map/concatenate | solution.py:133
  231.6 0.8 convolution_add_fusion
  232.8 1.9 fusion.10
  234.7 2.8 fusion.35
  237.6 7.7 %fusion.36 = f32[2048,256]{1,0:T(8,128)S(1)} fusion(f32[2048,768]{1,0:T(8,128)} %all-reduce.12.cloned.1.call-done, f32[128,128]{1,0:T(8,128)S(1)} %copy.27, f32[128,128]{1,0:T(8,128)} %copy-done.6, f32[128,256]{1,0:T(8,128)S(1)} %concatenate.108, f32[256,256]{1,0:T(8,128)S(1)} %convolution_negate_fusion, f32[256,256]{1,0:T(8,128)S(1)} %convolution_negate_fusion.1), kind=kOutput, calls=%fused_computation.78 | convolution fusion | flops 4832624640 | bytes 9175040 | tf_op jit(solution)/shard_map/dot_general | solution.py:147
  245.3 3.7 %fusion = f32[2048,256]{1,0:T(8,128)S(1)} fusion(f32[2048,768]{1,0:T(8,128)S(1)} %copy-done, f32[128,128]{1,0:T(8,128)S(1)} %copy.17, f32[128,128]{1,0:T(8,128)S(1)} %convolution_negate_fusion.4, f32[128,256]{1,0:T(8,128)S(1)} %concatenate.99, f32[256,256]{1,0:T(8,128)S(1)} %convolution_negate_fusion.2), kind=kOutput, calls=%fused_computation.2 | convolution fusion | flops 3221618688 | bytes 6815744 | tf_op jit(solution)/shard_map/dot_general | solution.py:147
  249.0 1.9 fusion.12
  251.0 1.5 maximum_select_fusion
  252.5 0.7 slice-done.1
  253.5 23.2 %subtract_select_fusion = f32[2048,1024]{1,0:T(8,128)} fusion(f32[2048,1024]{1,0:T(8,128)S(1)} %bitcast.95, pred[1024]{0:T(1024)(128)(4,1)S(1)} %fusion.83, pred[2048]{0:T(1024)(128)(4,1)S(1)} %fusion.76, f32[2048,768]{1,0:T(8,128)S(1)} %maximum_select_fusion, f32[256,1024]{1,0:T(8,128)S(1)} %fusion.35, f32[256,1024]{1,0:T(8,128)S(1)} %fusion.10, ...), kind=kOutput, calls=%fused_computation | convolution fusion | flops 19335217152 | bytes 26217472 | tf_op jit(solution)/shard_map/dot_general | solution.py:182
  (127 shorter events, 17.5 us)
Async XLA Ops:
  7.2 108.9 %all-reduce.14.cloned.1.call-start = ((), (), s32[]{:S(2)}) async-start(), calls=%async_computation.1 | async-start | bytes 6291456 | tf_op jit(solution)/shard_map/psum | solution.py:83
  8.9 1.7 copy-start.3
  10.6 226.9 %all-reduce.12.cloned.1.call-start = ((), (), s32[]{:S(2)}) async-start(), calls=%async_computation | async-start | bytes 12582912 | tf_op jit(solution)/shard_map/psum | solution.py:74
  11.6 2.2 collective-permute-start.2
  12.3 1.5 collective-permute-start.1
  13.0 0.8 collective-permute-start
  15.0 10.9 %collective-permute-start.5 = (f32[256,256]{1,0:T(8,128)S(1)}, f32[256,256]{1,0:T(8,128)S(1)}, u32[]{:S(2)}, u32[]{:S(2)}) collective-permute-start(f32[256,256]{1,0:T(8,128)S(1)} %get-tuple-element.20), channel_id=1, source_target_pairs={{0,12},{1,13},{2,14},{3,15}} | collective-permute-start | bytes 786440 | tf_op jit(solution)/shard_map/ppermute | solution.py:47
  15.7 11.5 %collective-permute-start.4 = (f32[256,256]{1,0:T(8,128)S(1)}, f32[256,256]{1,0:T(8,128)S(1)}, u32[]{:S(2)}, u32[]{:S(2)}) collective-permute-start(f32[256,256]{1,0:T(8,128)S(1)} %get-tuple-element.20), channel_id=1, source_target_pairs={{0,8},{1,9},{2,10},{3,11}} | collective-permute-start | bytes 786440 | tf_op jit(solution)/shard_map/ppermute | solution.py:47
  16.3 10.8 %collective-permute-start.3 = (f32[256,256]{1,0:T(8,128)S(1)}, f32[256,256]{1,0:T(8,128)S(1)}, u32[]{:S(2)}, u32[]{:S(2)}) collective-permute-start(f32[256,256]{1,0:T(8,128)S(1)} %get-tuple-element.20), channel_id=1, source_target_pairs={{0,4},{1,5},{2,6},{3,7}} | collective-permute-start | bytes 786440 | tf_op jit(solution)/shard_map/ppermute | solution.py:47
  23.6 30.3 %collective-permute-start.12 = (f32[256,768]{1,0:T(8,128)S(1)}, f32[256,768]{1,0:T(8,128)S(1)}, u32[]{:S(2)}, u32[]{:S(2)}) collective-permute-start(f32[256,768]{1,0:T(8,128)S(1)} %fusion.18), channel_id=1, source_target_pairs={{16,28},{17,29},{18,30},{19,31},{32,44},{33,45},{34,46},{35,47}} | collective-permute-start | bytes 2359304 | tf_op jit(solution)/shard_map/ppermute | solution.py:47
  24.3 29.6 %collective-permute-start.11 = (f32[256,768]{1,0:T(8,128)S(1)}, f32[256,768]{1,0:T(8,128)}, u32[]{:S(2)}, u32[]{:S(2)}) collective-permute-start(f32[256,768]{1,0:T(8,128)S(1)} %fusion.18), channel_id=1, source_target_pairs={{16,24},{17,25},{18,26},{19,27},{32,40},{33,41},{34,42},{35,43}} | collective-permute-start | bytes 2359304 | tf_op jit(solution)/shard_map/ppermute | solution.py:47
  25.8 32.7 %collective-permute-start.10 = (f32[256,768]{1,0:T(8,128)S(1)}, f32[256,768]{1,0:T(8,128)}, u32[]{:S(2)}, u32[]{:S(2)}) collective-permute-start(f32[256,768]{1,0:T(8,128)S(1)} %fusion.18), channel_id=1, source_target_pairs={{16,20},{17,21},{18,22},{19,23},{32,36},{33,37},{34,38},{35,39}} | collective-permute-start | bytes 2359304 | tf_op jit(solution)/shard_map/ppermute | solution.py:47
  27.2 1.6 collective-permute-start.8
  28.2 3.4 %collective-permute-start.7 = (f32[256,256]{1,0:T(8,128)S(1)}, f32[256,256]{1,0:T(8,128)S(1)}, u32[]{:S(2)}, u32[]{:S(2)}) collective-permute-start(f32[256,256]{1,0:T(8,128)S(1)} %select_add_fusion.5), channel_id=1, source_target_pairs={{0,64},{1,65},{2,66},{3,67},{4,68},{5,69},{6,70},{7,71},{8,72},{9,... | collective-permute-start | bytes 786440 | tf_op jit(solution)/shard_map/ppermute | solution.py:57
  28.9 24.8 %collective-permute-start.6 = (f32[256,256]{1,0:T(8,128)S(1)}, f32[256,256]{1,0:T(8,128)S(1)}, u32[]{:S(2)}, u32[]{:S(2)}) collective-permute-start(f32[256,256]{1,0:T(8,128)S(1)} %select_add_fusion.5), channel_id=1, source_target_pairs={{0,32},{1,33},{2,34},{3,35},{4,36},{5,37},{6,38},{7,39},{8,40},{9,... | collective-permute-start | bytes 786440 | tf_op jit(solution)/shard_map/ppermute | solution.py:57
  53.8 12.0 %collective-permute-start.9 = (f32[256,256]{1,0:T(8,128)S(1)}, f32[256,256]{1,0:T(8,128)S(1)}, u32[]{:S(2)}, u32[]{:S(2)}) collective-permute-start(f32[256,256]{1,0:T(8,128)S(1)} %select_add_fusion.4), channel_id=1, source_target_pairs={{0,16},{1,17},{2,18},{3,19},{4,20},{5,21},{6,22},{7,23},{8,24},{9,... | collective-permute-start | bytes 786440 | tf_op jit(solution)/shard_map/ppermute | solution.py:61
  59.9 53.5 %collective-permute-start.15 = (f32[256,768]{1,0:T(8,128)S(1)}, f32[256,768]{1,0:T(8,128)S(1)}, u32[]{:S(2)}, u32[]{:S(2)}) collective-permute-start(f32[256,768]{1,0:T(8,128)S(1)} %select_add_fusion.1), channel_id=1, source_target_pairs={{16,112},{17,113},{18,114},{19,115},{20,116},{21,117},{22,118},{23... | collective-permute-start | bytes 2359304 | tf_op jit(solution)/shard_map/ppermute | solution.py:57
  61.3 52.2 %collective-permute-start.14 = (f32[256,768]{1,0:T(8,128)S(1)}, f32[256,768]{1,0:T(8,128)}, u32[]{:S(2)}, u32[]{:S(2)}) collective-permute-start(f32[256,768]{1,0:T(8,128)S(1)} %select_add_fusion.1), channel_id=1, source_target_pairs={{16,80},{17,81},{18,82},{19,83},{20,84},{21,85},{22,86},{23,87},{2... | collective-permute-start | bytes 2359304 | tf_op jit(solution)/shard_map/ppermute | solution.py:57
  63.4 50.9 %collective-permute-start.13 = (f32[256,768]{1,0:T(8,128)S(1)}, f32[256,768]{1,0:T(8,128)}, u32[]{:S(2)}, u32[]{:S(2)}) collective-permute-start(f32[256,768]{1,0:T(8,128)S(1)} %select_add_fusion.1), channel_id=1, source_target_pairs={{16,48},{17,49},{18,50},{19,51},{20,52},{21,53},{22,54},{23,55},{2... | collective-permute-start | bytes 2359304 | tf_op jit(solution)/shard_map/ppermute | solution.py:57
  113.5 0.9 copy-start.10
  114.6 4.7 %collective-permute-start.16 = (f32[256,768]{1,0:T(8,128)S(1)}, f32[256,768]{1,0:T(8,128)}, u32[]{:S(2)}, u32[]{:S(2)}) collective-permute-start(f32[256,768]{1,0:T(8,128)S(1)} %select_add_fusion), channel_id=1, source_target_pairs={{0,16},{1,17},{2,18},{3,19},{4,20},{5,21},{6,22},{7,23},{8,24},{9,... | collective-permute-start | bytes 2359304 | tf_op jit(solution)/shard_map/ppermute | solution.py:61
  175.0 50.2 %copy-start.7 = (f32[256,256]{1,0:T(8,128)S(1)}, f32[256,256]{1,0:T(8,128)}, u32[]{:S(2)}) copy-start(f32[256,256]{1,0:T(8,128)} %select_maximum_fusion.1) | copy-start | bytes 786436
  175.7 49.6 %copy-start.8 = (f32[256,256]{1,0:T(8,128)S(1)}, f32[256,256]{1,0:T(8,128)}, u32[]{:S(2)}) copy-start(f32[256,256]{1,0:T(8,128)} %copy.15) | copy-start | bytes 786436
  175.7 49.6 %copy-start.9 = (f32[256,256]{1,0:T(8,128)S(1)}, f32[256,256]{1,0:T(8,128)}, u32[]{:S(2)}) copy-start(f32[256,256]{1,0:T(8,128)} %copy.23) | copy-start | bytes 786436
  228.4 4.3 %copy-start.2 = (f32[768,1024]{1,0:T(8,128)S(1)}, f32[768,1024]{1,0:T(8,128)}, u32[]{:S(2)}) copy-start(f32[768,1024]{1,0:T(8,128)} %all-reduce.14.cloned.1.call-done) | copy-start | bytes 9437188
  229.0 5.7 %copy-start.6 = (f32[128,128]{1,0:T(8,128)}, f32[128,128]{1,0:T(8,128)S(1)}, u32[]{:S(2)}) copy-start(f32[128,128]{1,0:T(8,128)S(1)} %convolution_negate_fusion.3) | copy-start | bytes 196612
  237.5 7.7 %copy-start = (f32[2048,768]{1,0:T(8,128)S(1)}, f32[2048,768]{1,0:T(8,128)}, u32[]{:S(2)}) copy-start(f32[2048,768]{1,0:T(8,128)} %all-reduce.12.cloned.1.call-done) | copy-start | bytes 18874372
  245.3 5.7 %copy-start.5 = (f32[256,768]{1,0:T(8,128)S(1)}, f32[256,768]{1,0:T(8,128)}, u32[]{:S(2)}) copy-start(f32[256,768]{1,0:T(8,128)} %fusion.24) | copy-start | bytes 2359300
  249.0 3.5 %slice-start = ((s8[8388608]{0:T(1024)(128)(4,1)}), s8[4194304]{0:T(1024)(128)(4,1)S(1)}, s32[]{:S(2)}) async-start(s8[8388608]{0:T(1024)(128)(4,1)} %bitcast.94), calls=%async_computation.2 | async-start | bytes 8388608
  251.0 2.2 slice-start.1
  251.0 2.5 copy-start.4
  253.5 23.2 %copy-start.1 = (f32[2048,768]{1,0:T(8,128)}, f32[2048,768]{1,0:T(8,128)S(1)}, u32[]{:S(2)}) copy-start(f32[2048,768]{1,0:T(8,128)S(1)} %maximum_select_fusion) | copy-start | bytes 18874372
Sparse Core Ops, SparseCore 0:
  10.9 78.9 all-reduce.13
  94.0 124.8 all-reduce.11

commit v4 on v3

--- a/solution.py
+++ b/solution.py
@@ -91,10 +91,10 @@
 def factor_block(schur):
     half = schur.shape[0] // 2
     eye = jnp.eye(half, dtype=jnp.float32)
-    top = jnp.linalg.cholesky(schur[:half, :half])
+    top = lax.linalg.cholesky(schur[:half, :half], symmetrize_input=False)
     top_inv = jax.scipy.linalg.solve_triangular(top, eye, lower=True)
     side = mul(schur[half:, :half], top_inv, True)
-    bottom = jnp.linalg.cholesky(schur[half:, half:] - mul(side, side, True))
+    bottom = lax.linalg.cholesky(schur[half:, half:] - mul(side, side, True), symmetrize_input=False)
     bottom_inv = jax.scipy.linalg.solve_triangular(bottom, eye, lower=True)
     corner = -mul(bottom_inv, mul(side, top_inv))
     zero = jnp.zeros((half, half), jnp.float32)

time: 289 us -> 289 us (level)
  the two profiles are of different devices: /device:TPU:10 before, /device:TPU:41 now
where the time goes in v4:
time: 289 us; the launch traced here: 285 us
  other arithmetic  155 us (54%)
  matrix products  58.5 us (20%)
  starting transfers between devices  37.9 us (13%)
  between operations  15.4 us (5%)
  local copies, waits for them, and re-layouts  11 us (4%)
  waiting for transfers between devices  6.96 us (2%)
    another operation x9, other arithmetic, factor_block(): lax.linalg.cholesky(schur[half:, half:] - mul(side, side, True), symmetri...  37.4 us
    another operation x9, other arithmetic, factor_block(): top = lax.linalg.cholesky(schur[:half, :half], symmetrize_input=False)  37.2 us
    another operation x6, other arithmetic, factor_block(): top_inv = jax.scipy.linalg.solve_triangular(top, eye, lower=True)  32.3 us
    another operation x6, other arithmetic, factor_block(): bottom_inv = jax.scipy.linalg.solve_triangular(bottom, eye, lower=True)  31.7 us
    dot_general x1, matrix products, shards(): lax.dot_general(panels, across, (((1,), (0,)), ((), ())), precision=lax.P...  23.2 us
    ppermute x2, starting transfers between devices, gather_corner(): other = lax.ppermute(held, ('row', 'col'), pairs)  22.3 us
    dot_general x3, matrix products, apply_inverse(): lax.dot_general(piece, inverse[j * BLOCK:hi, :hi], (((axis,), (1,)), ((),...  13.4 us
    dot_general x26, matrix products, mul(): lax.dot_general(a, b, dims, precision=lax.Precision.HIGHEST, preferred_el...  12.4 us
  transfers between devices with their start and end apart: 19, of which 1 were waited for; matrix products, arithmetic and copies ran while one was open for 64% of the time, Pallas kernels for 0%

profile of v4, /device:TPU:41, one launch (start us, length us, event | category | flops | bytes accessed | tf_op | source)
XLA Modules:
  0.0 285.0 jit_solution(9246254151987308888)
XLA Ops:
  7.6 1.3 select_dynamic-update-slice_fusion.1
  8.9 1.7 copy-done.3
  10.7 1.0 slice.73
  11.6 0.7 collective-permute-start.2
  12.3 0.7 collective-permute-start.1
  13.0 0.7 collective-permute-start
  13.8 1.1 select_add_fusion.2
  15.0 0.7 collective-permute-start.5
  15.7 0.7 collective-permute-start.4
  16.3 0.7 collective-permute-start.3
  17.0 3.1 %broadcast_in_dim.80 = f32[2048,768]{1,0:T(8,128)} broadcast(f32[]{:T(128)} %constant.239.clone.1), dimensions={} | broadcast | bytes 6291460 | tf_op jit(solution)/shard_map/broadcast_in_dim | solution.py:72
  20.1 3.2 %select_dynamic-update-slice_fusion = f32[2048,768]{1,0:T(8,128)} fusion(f32[2048,768]{1,0:T(8,128)} %broadcast_in_dim.80, s32[]{:T(128)S(6)} %select_n.512, f32[2048,1024]{1,0:T(8,128)} %param.4, pred[]{:T(512)S(6)} %lt.164), kind=kLoop, calls=%fused_computation.33 | loop fusion | flops 524288 | bytes 4194309 | tf_op jit(solution)/shard_map/dynamic_update_slice | solution.py:73
  23.6 0.7 collective-permute-start.12
  24.3 1.5 collective-permute-start.11
  25.8 1.3 collective-permute-start.10
  27.2 0.7 collective-permute-start.8
  28.2 0.7 collective-permute-start.7
  28.9 0.7 collective-permute-start.6
  29.6 1.4 iota_compare_fusion
  31.0 22.2 %collective-permute-start.9 = (f32[256,256]{1,0:T(8,128)S(1)}, f32[256,256]{1,0:T(8,128)S(1)}, u32[]{:S(2)}, u32[]{:S(2)}) collective-permute-start(f32[256,256]{1,0:T(8,128)S(1)} %select_add_fusion.4), channel_id=1, source_target_pairs={{0,16},{1,17},{2,18},{3,19},{4,20},{5,21},{6,22},{7,23},{8,24},{9,... | collective-permute-start | bytes 786440 | tf_op jit(solution)/shard_map/ppermute | solution.py:61
  53.2 6.8 %collective-permute-done.10 = f32[256,768]{1,0:T(8,128)} collective-permute-done((f32[256,768]{1,0:T(8,128)S(1)}, f32[256,768]{1,0:T(8,128)}, u32[]{:S(2)}, u32[]{:S(2)}) %collective-permute-start.10) | collective-permute-done | bytes 786464 | tf_op jit(solution)/shard_map/ppermute | solution.py:47
  60.1 1.3 select_add_fusion.1
  61.4 1.3 collective-permute-start.15
  62.8 2.2 collective-permute-start.14
  64.9 2.3 collective-permute-start.13
  67.3 11.7 %custom-call.16 = f32[128,128]{1,0:T(8,128)S(1)} custom-call(f32[128,128]{1,0:T(8,128)S(1)} %slice.94), custom_call_target="Cholesky" | custom-call | tf_op jit(solution)/shard_map/cholesky/custom-call.1 | solution.py:94
  80.3 9.8 %custom-call.17 = f32[1,128,128]{1,2,0:T(8,128)S(1)} custom-call(f32[1,128,128]{2,1,0:T(8,128)S(1)} %get-tuple-element.14), custom_call_target="InvertDiagBlocksLowerTriangular" | custom-call | tf_op jit(solution)/shard_map/jit(_solve_triangular)/triangular_solve | solution.py:95
  91.1 11.7 %custom-call.18 = f32[128,128]{1,0:T(8,128)S(1)} custom-call(f32[128,128]{1,0:T(8,128)S(1)} %slice_subtract_fusion.6), custom_call_target="Cholesky" | custom-call | tf_op jit(solution)/shard_map/cholesky/custom-call.1 | solution.py:97
  104.1 10.2 %custom-call.19 = f32[1,128,128]{1,2,0:T(8,128)S(1)} custom-call(f32[1,128,128]{2,1,0:T(8,128)S(1)} %get-tuple-element.12), custom_call_target="InvertDiagBlocksLowerTriangular" | custom-call | tf_op jit(solution)/shard_map/jit(_solve_triangular)/triangular_solve | solution.py:98
  114.6 0.9 copy-done.10
  115.7 0.7 select_maximum_fusion.1
  117.1 3.3 %fusion.14 = f32[256,1024]{1,0:T(8,128)} fusion(f32[768,1024]{1,0:T(8,128)} %all-reduce.14.cloned.1.call-done, f32[128,128]{1,0:T(8,128)S(1)} %fusion.53, f32[128,128]{1,0:T(8,128)S(1)} %copy.5, f32[128,128]{1,0:T(8,128)S(1)} %convolution_negate_fusion.5), kind=kOutput, calls=%fused_computation.41 | convolution fusion | flops 805568512 | bytes 2293760 | tf_op jit(solution)/shard_map/dot_general | solution.py:171
  120.4 1.2 broadcast_select_fusion.1
  122.7 11.7 %custom-call.20 = f32[128,128]{1,0:T(8,128)S(1)} custom-call(f32[128,128]{1,0:T(8,128)S(1)} %slice.99), custom_call_target="Cholesky" | custom-call | tf_op jit(solution)/shard_map/cholesky/custom-call.1 | solution.py:94
  134.4 0.7 compare_reduce_fusion.3
  135.1 1.3 select_bitcast_fusion.3
  136.4 9.8 %custom-call.21 = f32[1,128,128]{1,2,0:T(8,128)S(1)} custom-call(f32[1,128,128]{2,1,0:T(8,128)S(1)} %get-tuple-element.10), custom_call_target="InvertDiagBlocksLowerTriangular" | custom-call | tf_op jit(solution)/shard_map/jit(_solve_triangular)/triangular_solve | solution.py:95
  147.7 11.9 %custom-call.22 = f32[128,128]{1,0:T(8,128)S(1)} custom-call(f32[128,128]{1,0:T(8,128)S(1)} %slice_subtract_fusion.5), custom_call_target="Cholesky" | custom-call | tf_op jit(solution)/shard_map/cholesky/custom-call.1 | solution.py:97
  159.7 0.7 compare_reduce_fusion.2
  160.3 0.6 select_bitcast_fusion.2
  161.0 9.8 %custom-call.23 = f32[1,128,128]{1,2,0:T(8,128)S(1)} custom-call(f32[1,128,128]{2,1,0:T(8,128)S(1)} %get-tuple-element.8), custom_call_target="InvertDiagBlocksLowerTriangular" | custom-call | tf_op jit(solution)/shard_map/jit(_solve_triangular)/triangular_solve | solution.py:98
  171.1 0.8 copy.7
  172.1 0.8 copy.11
  174.3 0.8 copy.12
  176.3 11.7 %custom-call.24 = f32[128,128]{1,0:T(8,128)S(1)} custom-call(f32[128,128]{1,0:T(8,128)S(1)} %slice.105), custom_call_target="Cholesky" | custom-call | tf_op jit(solution)/shard_map/cholesky/custom-call.1 | solution.py:94
  188.1 0.7 compare_reduce_fusion.1
  188.8 0.6 select_bitcast_fusion.1
  189.4 10.2 %custom-call.25 = f32[1,128,128]{1,2,0:T(8,128)S(1)} custom-call(f32[1,128,128]{2,1,0:T(8,128)S(1)} %get-tuple-element.6), custom_call_target="InvertDiagBlocksLowerTriangular" | custom-call | tf_op jit(solution)/shard_map/jit(_solve_triangular)/triangular_solve | solution.py:95
  199.9 1.1 fusion.56
  201.1 1.1 slice_subtract_fusion.4
  202.3 11.7 %custom-call.26 = f32[128,128]{1,0:T(8,128)S(1)} custom-call(f32[128,128]{1,0:T(8,128)S(1)} %slice_subtract_fusion.4), custom_call_target="Cholesky" | custom-call | tf_op jit(solution)/shard_map/cholesky/custom-call.1 | solution.py:97
  214.0 0.7 compare_reduce_fusion
  214.7 0.6 select_bitcast_fusion
  215.3 9.8 %custom-call.27 = f32[1,128,128]{1,2,0:T(8,128)S(1)} custom-call(f32[1,128,128]{2,1,0:T(8,128)S(1)} %get-tuple-element.4), custom_call_target="InvertDiagBlocksLowerTriangular" | custom-call | tf_op jit(solution)/shard_map/jit(_solve_triangular)/triangular_solve | solution.py:98
  225.5 1.0 pad_select_fusion
  226.6 3.1 %fusion.24 = f32[256,768]{1,0:T(8,128)} fusion(s32[]{:T(128)S(6)} %select_n.509, f32[256,256]{1,0:T(8,128)} %copy.7, f32[128,128]{1,0:T(8,128)S(1)} %copy.6, f32[128,128]{1,0:T(8,128)S(1)} %get-tuple-element.9, f32[256,256]{1,0:T(8,128)S(1)} %broadcast_in_dim.78, f32[256,256]{1,0:T(8,128)} %copy.11, f32[256,256]{1,0:T(8,128)S(1)} %copy-done.8, ...), kind=kLoop, calls=%fused_computation.55 | loop fusion | flops 3735552 | bytes 3802112 | tf_op jit(solution)/shard_map/concatenate | solution.py:133
  234.0 1.9 fusion.10
  236.0 2.8 fusion.35
  238.8 7.7 %fusion.36 = f32[2048,256]{1,0:T(8,128)S(1)} fusion(f32[2048,768]{1,0:T(8,128)} %all-reduce.12.cloned.1.call-done, f32[128,128]{1,0:T(8,128)S(1)} %copy.15, f32[128,128]{1,0:T(8,128)} %copy-done.6, f32[128,256]{1,0:T(8,128)S(1)} %concatenate.108, f32[256,256]{1,0:T(8,128)S(1)} %convolution_negate_fusion, f32[256,256]{1,0:T(8,128)S(1)} %convolution_negate_fusion.1), kind=kOutput, calls=%fused_computation.78 | convolution fusion | flops 4832624640 | bytes 9175040 | tf_op jit(solution)/shard_map/dot_general | solution.py:147
  246.6 3.7 %fusion = f32[2048,256]{1,0:T(8,128)S(1)} fusion(f32[2048,768]{1,0:T(8,128)S(1)} %copy-done, f32[128,128]{1,0:T(8,128)S(1)} %copy.9, f32[128,128]{1,0:T(8,128)S(1)} %convolution_negate_fusion.4, f32[128,256]{1,0:T(8,128)S(1)} %concatenate.99, f32[256,256]{1,0:T(8,128)S(1)} %convolution_negate_fusion.2), kind=kOutput, calls=%fused_computation.2 | convolution fusion | flops 3221618688 | bytes 6815744 | tf_op jit(solution)/shard_map/dot_general | solution.py:147
  250.3 1.9 fusion.12
  252.3 1.5 maximum_select_fusion
  253.8 0.7 slice-done.1
  254.7 23.2 %subtract_select_fusion = f32[2048,1024]{1,0:T(8,128)} fusion(f32[2048,1024]{1,0:T(8,128)S(1)} %bitcast.71, pred[1024]{0:T(1024)(128)(4,1)S(1)} %fusion.77, pred[2048]{0:T(1024)(128)(4,1)S(1)} %fusion.70, f32[2048,768]{1,0:T(8,128)S(1)} %maximum_select_fusion, f32[256,1024]{1,0:T(8,128)S(1)} %fusion.35, f32[256,1024]{1,0:T(8,128)S(1)} %fusion.10, ...), kind=kOutput, calls=%fused_computation | convolution fusion | flops 19335217152 | bytes 26217472 | tf_op jit(solution)/shard_map/dot_general | solution.py:182
  (109 shorter events, 16.6 us)
Async XLA Ops:
  7.2 110.0 %all-reduce.14.cloned.1.call-start = ((), (), s32[]{:S(2)}) async-start(), calls=%async_computation.1 | async-start | bytes 6291456 | tf_op jit(solution)/shard_map/psum | solution.py:83
  8.9 1.7 copy-start.3
  10.6 228.2 %all-reduce.12.cloned.1.call-start = ((), (), s32[]{:S(2)}) async-start(), calls=%async_computation | async-start | bytes 12582912 | tf_op jit(solution)/shard_map/psum | solution.py:74
  11.6 2.2 collective-permute-start.2
  12.3 1.5 collective-permute-start.1
  13.0 0.8 collective-permute-start
  15.0 10.9 %collective-permute-start.5 = (f32[256,256]{1,0:T(8,128)S(1)}, f32[256,256]{1,0:T(8,128)S(1)}, u32[]{:S(2)}, u32[]{:S(2)}) collective-permute-start(f32[256,256]{1,0:T(8,128)S(1)} %get-tuple-element.20), channel_id=1, source_target_pairs={{0,12},{1,13},{2,14},{3,15}} | collective-permute-start | bytes 786440 | tf_op jit(solution)/shard_map/ppermute | solution.py:47
  15.7 11.5 %collective-permute-start.4 = (f32[256,256]{1,0:T(8,128)S(1)}, f32[256,256]{1,0:T(8,128)S(1)}, u32[]{:S(2)}, u32[]{:S(2)}) collective-permute-start(f32[256,256]{1,0:T(8,128)S(1)} %get-tuple-element.20), channel_id=1, source_target_pairs={{0,8},{1,9},{2,10},{3,11}} | collective-permute-start | bytes 786440 | tf_op jit(solution)/shard_map/ppermute | solution.py:47
  16.3 10.8 %collective-permute-start.3 = (f32[256,256]{1,0:T(8,128)S(1)}, f32[256,256]{1,0:T(8,128)S(1)}, u32[]{:S(2)}, u32[]{:S(2)}) collective-permute-start(f32[256,256]{1,0:T(8,128)S(1)} %get-tuple-element.20), channel_id=1, source_target_pairs={{0,4},{1,5},{2,6},{3,7}} | collective-permute-start | bytes 786440 | tf_op jit(solution)/shard_map/ppermute | solution.py:47
  23.6 29.7 %collective-permute-start.12 = (f32[256,768]{1,0:T(8,128)S(1)}, f32[256,768]{1,0:T(8,128)S(1)}, u32[]{:S(2)}, u32[]{:S(2)}) collective-permute-start(f32[256,768]{1,0:T(8,128)S(1)} %fusion.18), channel_id=1, source_target_pairs={{16,28},{17,29},{18,30},{19,31},{32,44},{33,45},{34,46},{35,47}} | collective-permute-start | bytes 2359304 | tf_op jit(solution)/shard_map/ppermute | solution.py:47
  24.3 28.9 %collective-permute-start.11 = (f32[256,768]{1,0:T(8,128)S(1)}, f32[256,768]{1,0:T(8,128)}, u32[]{:S(2)}, u32[]{:S(2)}) collective-permute-start(f32[256,768]{1,0:T(8,128)S(1)} %fusion.18), channel_id=1, source_target_pairs={{16,24},{17,25},{18,26},{19,27},{32,40},{33,41},{34,42},{35,43}} | collective-permute-start | bytes 2359304 | tf_op jit(solution)/shard_map/ppermute | solution.py:47
  25.8 34.2 %collective-permute-start.10 = (f32[256,768]{1,0:T(8,128)S(1)}, f32[256,768]{1,0:T(8,128)}, u32[]{:S(2)}, u32[]{:S(2)}) collective-permute-start(f32[256,768]{1,0:T(8,128)S(1)} %fusion.18), channel_id=1, source_target_pairs={{16,20},{17,21},{18,22},{19,23},{32,36},{33,37},{34,38},{35,39}} | collective-permute-start | bytes 2359304 | tf_op jit(solution)/shard_map/ppermute | solution.py:47
  27.2 1.6 collective-permute-start.8
  28.2 2.8 collective-permute-start.7
  28.9 2.1 collective-permute-start.6
  31.0 36.3 %collective-permute-start.9 = (f32[256,256]{1,0:T(8,128)S(1)}, f32[256,256]{1,0:T(8,128)S(1)}, u32[]{:S(2)}, u32[]{:S(2)}) collective-permute-start(f32[256,256]{1,0:T(8,128)S(1)} %select_add_fusion.4), channel_id=1, source_target_pairs={{0,16},{1,17},{2,18},{3,19},{4,20},{5,21},{6,22},{7,23},{8,24},{9,... | collective-permute-start | bytes 786440 | tf_op jit(solution)/shard_map/ppermute | solution.py:61
  61.4 53.1 %collective-permute-start.15 = (f32[256,768]{1,0:T(8,128)S(1)}, f32[256,768]{1,0:T(8,128)S(1)}, u32[]{:S(2)}, u32[]{:S(2)}) collective-permute-start(f32[256,768]{1,0:T(8,128)S(1)} %select_add_fusion.1), channel_id=1, source_target_pairs={{16,112},{17,113},{18,114},{19,115},{20,116},{21,117},{22,118},{23... | collective-permute-start | bytes 2359304 | tf_op jit(solution)/shard_map/ppermute | solution.py:57
  62.8 51.8 %collective-permute-start.14 = (f32[256,768]{1,0:T(8,128)S(1)}, f32[256,768]{1,0:T(8,128)}, u32[]{:S(2)}, u32[]{:S(2)}) collective-permute-start(f32[256,768]{1,0:T(8,128)S(1)} %select_add_fusion.1), channel_id=1, source_target_pairs={{16,80},{17,81},{18,82},{19,83},{20,84},{21,85},{22,86},{23,87},{2... | collective-permute-start | bytes 2359304 | tf_op jit(solution)/shard_map/ppermute | solution.py:57
  64.9 50.5 %collective-permute-start.13 = (f32[256,768]{1,0:T(8,128)S(1)}, f32[256,768]{1,0:T(8,128)}, u32[]{:S(2)}, u32[]{:S(2)}) collective-permute-start(f32[256,768]{1,0:T(8,128)S(1)} %select_add_fusion.1), channel_id=1, source_target_pairs={{16,48},{17,49},{18,50},{19,51},{20,52},{21,53},{22,54},{23,55},{2... | collective-permute-start | bytes 2359304 | tf_op jit(solution)/shard_map/ppermute | solution.py:57
  114.5 0.9 copy-start.10
  115.6 4.8 %collective-permute-start.16 = (f32[256,768]{1,0:T(8,128)S(1)}, f32[256,768]{1,0:T(8,128)}, u32[]{:S(2)}, u32[]{:S(2)}) collective-permute-start(f32[256,768]{1,0:T(8,128)S(1)} %select_add_fusion), channel_id=1, source_target_pairs={{0,16},{1,17},{2,18},{3,19},{4,20},{5,21},{6,22},{7,23},{8,24},{9,... | collective-permute-start | bytes 2359304 | tf_op jit(solution)/shard_map/ppermute | solution.py:61
  175.1 51.4 %copy-start.7 = (f32[256,256]{1,0:T(8,128)S(1)}, f32[256,256]{1,0:T(8,128)}, u32[]{:S(2)}) copy-start(f32[256,256]{1,0:T(8,128)} %select_maximum_fusion.1) | copy-start | bytes 786436
  176.3 13.1 %copy-start.9 = (f32[256,256]{1,0:T(8,128)}, f32[256,256]{1,0:T(8,128)S(1)}, u32[]{:S(2)}) copy-start(f32[256,256]{1,0:T(8,128)S(1)} %fusion.37) | copy-start | bytes 786436
  176.3 50.2 %copy-start.8 = (f32[256,256]{1,0:T(8,128)S(1)}, f32[256,256]{1,0:T(8,128)}, u32[]{:S(2)}) copy-start(f32[256,256]{1,0:T(8,128)} %copy.12) | copy-start | bytes 786436
  229.7 4.3 %copy-start.2 = (f32[768,1024]{1,0:T(8,128)S(1)}, f32[768,1024]{1,0:T(8,128)}, u32[]{:S(2)}) copy-start(f32[768,1024]{1,0:T(8,128)} %all-reduce.14.cloned.1.call-done) | copy-start | bytes 9437188
  230.3 5.7 %copy-start.6 = (f32[128,128]{1,0:T(8,128)}, f32[128,128]{1,0:T(8,128)S(1)}, u32[]{:S(2)}) copy-start(f32[128,128]{1,0:T(8,128)S(1)} %convolution_negate_fusion.3) | copy-start | bytes 196612
  238.8 7.7 %copy-start = (f32[2048,768]{1,0:T(8,128)S(1)}, f32[2048,768]{1,0:T(8,128)}, u32[]{:S(2)}) copy-start(f32[2048,768]{1,0:T(8,128)} %all-reduce.12.cloned.1.call-done) | copy-start | bytes 18874372
  246.6 5.7 %copy-start.5 = (f32[256,768]{1,0:T(8,128)S(1)}, f32[256,768]{1,0:T(8,128)}, u32[]{:S(2)}) copy-start(f32[256,768]{1,0:T(8,128)} %fusion.24) | copy-start | bytes 2359300
  250.3 3.5 %slice-start = ((s8[8388608]{0:T(1024)(128)(4,1)}), s8[4194304]{0:T(1024)(128)(4,1)S(1)}, s32[]{:S(2)}) async-start(s8[8388608]{0:T(1024)(128)(4,1)} %bitcast.70), calls=%async_computation.2 | async-start | bytes 8388608
  252.3 2.2 slice-start.1
  252.3 2.5 copy-start.4
  254.7 23.2 %copy-start.1 = (f32[2048,768]{1,0:T(8,128)}, f32[2048,768]{1,0:T(8,128)S(1)}, u32[]{:S(2)}) copy-start(f32[2048,768]{1,0:T(8,128)S(1)} %maximum_select_fusion) | copy-start | bytes 18874372
Sparse Core Ops, SparseCore 0:
  10.9 77.4 all-reduce.13
  92.5 124.8 all-reduce.11
